TPU v7x, 32 devices: a whole 2x2x4 slice. The times are simulated.
32 devices in a mesh: tm: 8 (over z, x), height: 2 (over core), batch: 2 (over y).
Axes of the slice: x: 2, y: 2, z: 4, core: 2. Of those that a mesh axis runs over, the one named last changes fastest.
Arguments:
- inputs: float32 [2, 32, 4, 160, 96], P('batch', 'tm', 'height'), may hold values from -6 to 6
- weight_one: float32 [3, 3, 3, 96, 96], replicated, may hold values from -0.125 to 0.125
- bias_one: float32 [96], replicated, may hold values from -4 to 4
- gain_one: float32 [96], replicated, may hold values from 0.25 to 1.75
- weight_two: float32 [3, 3, 3, 96, 96], replicated, may hold values from -0.125 to 0.125
- gain_two: float32 [96], replicated, may hold values from 0.25 to 1.75
- cotangent: float32 [2, 32, 4, 160, 96], P('batch', 'tm', 'height'), may hold values from -6 to 6
Outputs:
- grad_inputs: float32 [2, 32, 4, 160, 96], P('batch', 'tm', 'height')
- grad_weight_one: float32 [2592, 96], P('tm')
- grad_weight_two: float32 [2592, 96], P('tm')
- grad_vectors: float32 [4, 96], replicated
All inputs are finite; a program needn't handle non-finite values.
Results may differ from a plain program's by a relative error of at most 0.00012.
Values sent between devices are 32-bit elements; how exact they have to be, the bound alone decides.
No kernel may reach another device: no remote copies, remote signals or barrier semaphores. Data moves between devices by JAX's collectives and lax.ppermute only.
A program may use at most 128 MiB of HBM per device.

v0:
```python
import math

import jax
import jax.numpy as jnp
from jax import lax
from jax.sharding import PartitionSpec as P


def passed_along(block, axis, distance):
    devices = range(lax.axis_size(axis))
    route = [(i - distance, i) for i in devices if i - distance in devices]
    return lax.ppermute(block, axis, route)


def padded(block, sides, width):
    for axis, dim in sides:
        count = lax.axis_size(axis)
        top = lax.slice_in_dim(block, block.shape[dim] - width, None, axis=dim)
        bottom = lax.slice_in_dim(block, 0, width, axis=dim)
        if count == 2:
            first = lax.axis_index(axis) == 0
            got = lax.ppermute(jnp.where(first, top, bottom), axis, [(0, 1), (1, 0)])
            empty = jnp.zeros_like(got)
            low = jnp.where(first, empty, got)
            high = jnp.where(first, got, empty)
        else:
            forward = [(i, i + 1) for i in range(count - 1)]
            backward = [(target, source) for source, target in forward]
            low = lax.ppermute(top, axis, forward)
            high = lax.ppermute(bottom, axis, backward)
        block = jnp.concatenate([low, block, high], axis=dim)
    return block


def norm_act(values, scales):
    square = jnp.mean(values * values, axis=-1, keepdims=True)
    return jax.nn.silu(values * lax.rsqrt(square + 1e-06) * scales)


def row_patches(wide):
    frames = wide.shape[1] - 2
    rows = wide.shape[2] - 2
    edged = jnp.pad(wide, ((0, 0), (0, 0), (0, 0), (1, 1), (0, 0)))
    pieces = [edged[:, i : i + frames, j : j + rows] for i in range(3) for j in range(3)]
    taps = jnp.concatenate(pieces, axis=-1)
    return taps.reshape(-1, taps.shape[-1])


def conv_rows(taps, kernel, shape):
    cols = shape[3]
    width = kernel.shape[-1]
    stacked = jnp.concatenate([kernel[:, :, l].reshape(-1, width) for l in range(3)], axis=1)
    out = jnp.dot(taps, stacked, precision=lax.Precision.HIGH)
    out = out.reshape(tuple(shape[:3]) + (cols + 2, 3 * width))
    return sum(out[:, :, :, l : l + cols, l * width : (l + 1) * width] for l in range(3))


def shifted_columns(values):
    return jnp.concatenate(
        [jnp.pad(values, ((0, 0), (0, 0), (0, 0), (l, 2 - l), (0, 0))) for l in range(3)], axis=-1
    )


def kernel_grad_rows(taps, grad):
    width = grad.shape[-1]
    flat = lax.optimization_barrier(shifted_columns(grad).reshape(-1, 3 * width).T)
    spread = lax.optimization_barrier(jnp.dot(flat, taps, precision=lax.Precision.HIGH))
    spread = spread.reshape(3, width, 3, 3, -1)
    return jnp.transpose(spread, (2, 3, 0, 4, 1)).reshape(-1, width)


def kernel_grad_rows_flipped(values, taps):
    channels = values.shape[-1]
    flat = lax.optimization_barrier(shifted_columns(values).reshape(-1, 3 * channels).T)
    spread = lax.optimization_barrier(jnp.dot(flat, taps, precision=lax.Precision.HIGH))
    spread = spread.reshape(3, channels, 3, 3, -1)[::-1, :, ::-1, ::-1]
    return jnp.transpose(spread, (2, 3, 0, 1, 4)).reshape(27 * channels, -1)


def flipped(kernel):
    return jnp.swapaxes(kernel[::-1, ::-1, ::-1], 3, 4)


def exchanged(block, axis, bit):
    count = lax.axis_size(axis)
    return lax.ppermute(block, axis, [(i, i ^ bit) for i in range(count)])


def halved(blocks, axis):
    count = lax.axis_size(axis)
    if count & (count - 1):
        return lax.psum_scatter(blocks, axis, scatter_dimension=0)
    me = lax.axis_index(axis)
    bit = 1
    while bit < count:
        mine = (me // bit) % 2
        pairs = blocks.reshape((blocks.shape[0] // 2, 2) + blocks.shape[1:])
        keep = lax.dynamic_index_in_dim(pairs, mine, axis=1, keepdims=False)
        send = lax.dynamic_index_in_dim(pairs, 1 - mine, axis=1, keepdims=False)
        blocks = keep + exchanged(send, axis, bit)
        bit *= 2
    return blocks[0]


def summed(block, axis):
    count = lax.axis_size(axis)
    if count & (count - 1):
        return lax.psum(block, axis)
    bit = 1
    while bit < count:
        block = block + exchanged(block, axis, bit)
        bit *= 2
    return block


def gathered(block, axis):
    count = lax.axis_size(axis)
    if count & (count - 1):
        return lax.all_gather(block, axis, tiled=True)
    me = lax.axis_index(axis)
    bit = 1
    while bit < count:
        other = exchanged(block, axis, bit)
        low = (me // bit) % 2 == 0
        block = jnp.where(low, jnp.concatenate([block, other]), jnp.concatenate([other, block]))
        bit *= 2
    return block


def reduced(blocks):
    parts, size, channels = blocks.shape
    split = lax.axis_size("height")
    width = -(-size // split)
    blocks = jnp.pad(blocks, ((0, 0), (0, width * split - size), (0, 0)))
    blocks = jnp.swapaxes(blocks.reshape(parts, split, width, channels), 0, 1)
    block = halved(halved(blocks, "height"), "tm")
    return gathered(summed(block, "batch"), "height")[:size]


def on_device(inputs, weight_one, bias_one, gain_one, weight_two, gain_two, cotangent):
    frames = inputs.shape[1]
    rows = inputs.shape[2]
    acts = norm_act(inputs, gain_one)
    acts_past = passed_along(acts[:, frames - 2 :], "tm", 1)
    cot_next = passed_along(cotangent[:, :2], "tm", -1)
    both = jnp.concatenate(
        [jnp.concatenate([acts_past, acts], axis=1), jnp.concatenate([cotangent, cot_next], axis=1)]
    )
    both = padded(both, (("height", 2),), 1)
    acts_wide = both[: inputs.shape[0]]
    cot_wide = both[inputs.shape[0] :]
    acts_taps = row_patches(acts_wide)
    hidden = conv_rows(acts_taps, weight_one, inputs.shape) + bias_one
    gated = norm_act(hidden, gain_two)
    cot_taps = row_patches(cot_wide)
    grad_gated = conv_rows(cot_taps, flipped(weight_two), inputs.shape)
    flat_two = kernel_grad_rows_flipped(gated, cot_taps)
    _, pull_norm_two = jax.vjp(norm_act, hidden, gain_two)
    grad_hidden, gain_two_part = pull_norm_two(grad_gated)
    grad_next = passed_along(grad_hidden[:, :2], "tm", -1)
    grad_wide = padded(jnp.concatenate([grad_hidden, grad_next], axis=1), (("height", 2),), 1)
    grad_acts = conv_rows(row_patches(grad_wide), flipped(weight_one), inputs.shape)
    flat_one = kernel_grad_rows(acts_taps, grad_hidden)
    _, pull_norm_one = jax.vjp(norm_act, inputs, gain_one)
    grad_part, gain_one_part = pull_norm_one(grad_acts)
    grad_inputs = cotangent + grad_part
    channels = flat_one.shape[1]
    taps = flat_one.shape[0]
    count = (
        inputs.shape[0]
        * frames
        * rows
        * inputs.shape[3]
        * lax.axis_size("tm")
        * lax.axis_size("height")
        * lax.axis_size("batch")
    )
    factor = 1.0 / math.sqrt(count)
    parts = lax.axis_size("tm")
    share = taps // parts
    vectors = jnp.stack(
        [
            jnp.sum(grad_hidden, axis=(0, 1, 2, 3)),
            jnp.sum(cotangent, axis=(0, 1, 2, 3)),
            gain_one_part,
            gain_two_part,
        ]
    )
    packed = jnp.concatenate(
        [
            flat_one.reshape(parts, share, channels),
            flat_two.reshape(parts, share, channels),
            jnp.broadcast_to(vectors, (parts,) + vectors.shape),
        ],
        axis=1,
    )
    total = reduced(packed * factor)
    return (grad_inputs, total[:share], total[share : 2 * share], total[2 * share :])


def solution(mesh):
    placed = (
        P("batch", "tm", "height", None, None),
        P(),
        P(),
        P(),
        P(),
        P(),
        P("batch", "tm", "height", None, None),
    )
    return jax.shard_map(
        on_device,
        mesh=mesh,
        in_specs=placed,
        out_specs=(P("batch", "tm", "height", None, None), P("tm", None), P("tm", None), P()),
        check_vma=False,
    )
```

profile of v0, /device:TPU:0, one launch (start us, length us, event | category | flops | bytes accessed | tf_op | source)
XLA Modules:
  0.0 206.4 jit_solution(11336747894402350021)
XLA Ops:
  3.6 4.9 %collective-permute-start = (f32[1,2,2,160,96]{4,3,2,1,0:T(8,128)S(1)}, f32[1,2,2,160,96]{4,3,2,1,0:T(8,128)S(1)}, u32[]{:S(2)}, u32[]{:S(2)}) collective-permute-start(f32[1,2,2,160,96]{4,3,2,1,0:T(8,128)S(1)} %slice.228), channel_id=1, source_target_pairs={{0,4},{4,8},{8,12},{12,16},{16,20},{20,24},{24,28},{1,5},{5,9},{9,... | collective-permute-start | bytes 737288 | tf_op jit(solution)/shard_map/ppermute | solution.py:12
  10.7 11.8 %collective-permute-done = f32[1,2,2,160,96]{4,3,2,1,0:T(8,128)S(1)} collective-permute-done((f32[1,2,2,160,96]{4,3,2,1,0:T(8,128)S(1)}, f32[1,2,2,160,96]{4,3,2,1,0:T(8,128)S(1)}, u32[]{:S(2)}, u32[]{:S(2)}) %collective-permute-start) | collective-permute-done | bytes 245792 | tf_op jit(solution)/shard_map/ppermute | solution.py:12
  32.9 1.9 copy.67
  34.9 1.9 copy.68
  44.8 4.1 %pad_slice_fusion = (f32[1,4,2,162,96]{4,3,2,1,0:T(8,128)}, f32[1,4,2,162,96]{4,3,2,1,0:T(8,128)}, f32[1,4,2,162,96]{4,3,2,1,0:T(8,128)}, f32[1,4,2,162,96]{4,3,...) fusion(f32[1,6,4,160,96]{4,3,2,1,0:T(8,128)S(1)} %get-tuple-ele, ...), kind=kLoop, calls=%fused_computation.27 | loop fusion | bytes 11907072 | tf_op jit(solution)/shard_map/slice | solution.py:44
  48.9 7.0 %concatenate.57 = f32[1,4,2,162,864]{4,3,2,1,0:T(8,128)} concatenate(f32[1,4,2,162,96]{4,3,2,1,0:T(8,128)} %get-tuple-element.60, f32[1,4,2,162,96]{4,3,2,1,0:T(8,128)} %get-tuple-element.53, f32[1,4,2,162,96]{4,3,2,1,0:T(8,128)} %get-tuple-element.54, f32[1,4,2,162,96]{4,3,2,1,0:T(8,128)} %get-tuple-element.55, f32[1,4,2,162,96]{4,3,2,1,0:T(8,128)} %get-tuple-element.56, ...), dimensions={4} | concatenate | bytes 8957952 | tf_op jit(solution)/shard_map/concatenate | solution.py:45
  55.9 4.2 %reshape.150 = f32[1296,864]{1,0:T(8,128)} reshape(f32[1,4,2,162,864]{4,3,2,1,0:T(8,128)} %concatenate.57) | data formatting | bytes 8957952 | tf_op jit(solution)/shard_map/reshape | solution.py:46
  60.1 6.2 %fusion.11 = f32[1,4,2,162,288]{4,3,2,1,0:T(8,128)S(1)} fusion(f32[1,4,2,162,864]{4,3,2,1,0:T(8,128)} %concatenate.57, f32[864,96]{0,1:T(8,128)S(1)} %copy-done.9, f32[864,96]{0,1:T(8,128)S(1)} %copy-done.8, f32[864,96]{0,1:T(8,128)S(1)} %copy-done.7), kind=kOutput, calls=%fused_computation.25 | convolution fusion | flops 1935415296 | bytes 6967296 | tf_op jit(solution)/shard_map/dot_general | solution.py:53
  67.1 6.8 %concatenate.55 = f32[1,4,2,162,864]{4,3,2,1,0:T(8,128)} concatenate(f32[1,4,2,162,96]{4,3,2,1,0:T(8,128)S(1)} %get-tuple-element.79, f32[1,4,2,162,96]{4,3,2,1,0:T(8,128)} %get-tuple-element.86, f32[1,4,2,162,96]{4,3,2,1,0:T(8,128)} %get-tuple-element.85, f32[1,4,2,162,96]{4,3,2,1,0:T(8,128)} %get-tuple-element.84, f32[1,4,2,162,96]{4,3,2,1,0:T(8,128)} %get-tuple-element.83, ...), dimensions={4} | concatenate | bytes 8957952 | tf_op jit(solution)/shard_map/concatenate | solution.py:45
  73.9 6.4 %fusion.8 = f32[1,4,2,162,288]{4,3,2,1,0:T(8,128)S(1)} fusion(f32[1,4,2,162,864]{4,3,2,1,0:T(8,128)} %concatenate.55, f32[864,96]{0,1:T(8,128)} %copy.66, f32[864,96]{0,1:T(8,128)} %copy.65, f32[864,96]{0,1:T(8,128)S(1)} %copy-done.6), kind=kOutput, calls=%fused_computation.24 | convolution fusion | flops 1935415296 | bytes 6967296 | tf_op jit(solution)/shard_map/dot_general | solution.py:53
  87.2 6.9 %fusion.55 = f32[288,864]{1,0:T(8,128)} fusion(f32[288,1296]{0,1:T(8,128)} %bitcast.85, f32[1296,864]{1,0:T(8,128)} %reshape.150), kind=kOutput, calls=%fused_computation.127 | convolution fusion | flops 1934917632 | bytes 6967296 | tf_op jit(solution)/shard_map/dot_general | solution.py:67
  94.1 4.1 %reshape.153 = f32[1296,864]{1,0:T(8,128)} reshape(f32[1,4,2,162,864]{4,3,2,1,0:T(8,128)} %concatenate.55) | data formatting | bytes 8957952 | tf_op jit(solution)/shard_map/reshape | solution.py:46
  98.2 2.5 %reshape.151 = f32[3,96,3,3,96]{4,3,2,1,0:T(4,128)S(1)} reshape(f32[288,864]{1,0:T(8,128)} %fusion.55) | data formatting | bytes 1990656 | tf_op jit(solution)/shard_map/reshape | solution.py:68
  100.8 2.2 %copy.76 = f32[3,3,3,96,96]{4,3,2,1,0:T(8,128)} copy(f32[3,3,3,96,96]{3,1,0,4,2:T(4,128)S(1)} %bitcast.87) | data formatting | bytes 1990656 | tf_op jit(solution)/shard_map/transpose | solution.py:69
  105.8 2.6 %select_maximum_fusion = f32[1,4,2,162,288]{4,3,2,1,0:T(8,128)S(1)} fusion(f32[1,4,2,160,96]{4,3,2,1,0:T(8,128)} %get-tuple-element.72), kind=kLoop, calls=%fused_computation.12 | loop fusion | flops 3732480 | bytes 1984512 | tf_op jit(solution)/shard_map/concatenate | solution.py:59
  112.3 5.9 %fusion.56 = f32[288,864]{1,0:T(8,128)S(1)} fusion(f32[288,1296]{0,1:T(8,128)} %bitcast.84, f32[1296,864]{1,0:T(8,128)} %reshape.153), kind=kOutput, calls=%fused_computation.128 | convolution fusion | flops 1934917632 | bytes 6967296 | tf_op jit(solution)/shard_map/dot_general | solution.py:75
  118.3 2.2 %reshape.154 = f32[3,96,3,3,96]{4,3,2,1,0:T(4,128)} reshape(f32[288,864]{1,0:T(8,128)S(1)} %fusion.56) | data formatting | bytes 1990656 | tf_op jit(solution)/shard_map/reshape | solution.py:76
  120.4 6.5 %rev.11 = f32[3,96,3,3,96]{4,3,2,1,0:T(4,128)S(1)} reverse(f32[3,96,3,3,96]{4,3,2,1,0:T(4,128)} %reshape.154), dimensions={0,2,3} | reverse | bytes 1990656 | tf_op jit(solution)/shard_map/rev | solution.py:76
  133.4 2.0 fusion.49
  135.4 6.8 %concatenate.61 = f32[1,4,2,162,864]{4,3,2,1,0:T(8,128)} concatenate(f32[1,4,2,162,96]{4,3,2,1,0:T(8,128)} %get-tuple-element.42, f32[1,4,2,162,96]{4,3,2,1,0:T(8,128)} %get-tuple-element.41, f32[1,4,2,162,96]{4,3,2,1,0:T(8,128)} %get-tuple-element.40, f32[1,4,2,162,96]{4,3,2,1,0:T(8,128)} %get-tuple-element.39, f32[1,4,2,162,96]{4,3,2,1,0:T(8,128)} %get-tuple-element.38, ...), dimensions={4} | concatenate | bytes 8957952 | tf_op jit(solution)/shard_map/concatenate | solution.py:45
  142.2 6.7 %fusion.14 = f32[1,4,2,162,288]{4,3,2,1,0:T(8,128)S(1)} fusion(f32[1,4,2,162,864]{4,3,2,1,0:T(8,128)} %concatenate.61, f32[864,96]{0,1:T(8,128)} %copy.75, f32[864,96]{0,1:T(8,128)} %copy.74, f32[864,96]{0,1:T(8,128)S(1)} %copy-done.5), kind=kOutput, calls=%fused_computation.26 | convolution fusion | flops 1935415296 | bytes 6967296 | tf_op jit(solution)/shard_map/dot_general | solution.py:53
  151.8 2.0 maximum_multiply_fusion
  153.8 3.3 %mul.209 = f32[8,2,326,96]{2,1,3,0:T(2,128)S(1)} reshape(f32[8,652,96]{1,2,0:T(8,128)} %maximum_multiply_fusion) | data formatting | bytes 4005888 | tf_op jit(solution)/shard_map/mul | solution.py:197
  157.1 2.3 %constant_dynamic-slice_fusion.2 = (f32[8,1,326,96]{2,1,3,0:T(1,128)S(1)}, f32[8,1,326,96]{2,1,3,0:T(1,128)S(1)}) fusion(f32[8,2,326,96]{2,1,3,0:T(2,128)S(1)} %mul.209, s32[]{:T(128)S(6)} %select_n.109, s32[]{:T(128)S(6)} %select_n.110), kind=kLoop, calls=%fused_computation.115 | loop fusion | bytes 4005896 | tf_op jit(solution)/shard_map/dynamic-slice.4
  159.6 2.8 %collective-permute-done.5 = f32[1,8,326,96]{2,3,1,0:T(8,128)S(1)} collective-permute-done((f32[1,8,326,96]{2,3,1,0:T(8,128)S(1)}, f32[1,8,326,96]{2,3,1,0:T(8,128)S(1)}, u32[]{:S(2)}, u32[]{:S(2)}) %collective-permute-start.5) | collective-permute-done | bytes 1001504 | tf_op jit(solution)/shard_map/ppermute | solution.py:86
  162.6 3.2 %collective-permute-start.6 = (f32[4,326,96]{1,2,0:T(8,128)S(1)}, f32[4,326,96]{1,2,0:T(8,128)S(1)}, u32[]{:S(2)}, u32[]{:S(2)}) collective-permute-start(f32[4,326,96]{1,2,0:T(8,128)S(1)} %dynamic-slice_bitcast_fusion), channel_id=1, source_target_pairs={{0,4},{4,0},{8,12},{12,8},{16,20},{20,16},{24,28},{28,24},{1,5},{5... | collective-permute-start | bytes 1502216 | tf_op jit(solution)/shard_map/ppermute | solution.py:86
  165.8 13.6 %collective-permute-done.6 = f32[4,326,96]{1,2,0:T(8,128)S(1)} collective-permute-done((f32[4,326,96]{1,2,0:T(8,128)S(1)}, f32[4,326,96]{1,2,0:T(8,128)S(1)}, u32[]{:S(2)}, u32[]{:S(2)}) %collective-permute-start.6) | collective-permute-done | bytes 500768 | tf_op jit(solution)/shard_map/ppermute | solution.py:86
  179.5 3.1 %collective-permute-start.7 = (f32[2,326,96]{1,2,0:T(8,128)S(1)}, f32[2,326,96]{1,2,0:T(8,128)S(1)}, u32[]{:S(2)}, u32[]{:S(2)}) collective-permute-start(f32[2,326,96]{1,2,0:T(8,128)S(1)} %dynamic-slice_bitcast_fusion.1), channel_id=1, source_target_pairs={{0,8},{4,12},{8,0},{12,4},{16,24},{20,28},{24,16},{28,20},{1,9},{5... | collective-permute-start | bytes 751112 | tf_op jit(solution)/shard_map/ppermute | solution.py:86
  182.6 6.6 %collective-permute-done.7 = f32[2,326,96]{1,2,0:T(8,128)S(1)} collective-permute-done((f32[2,326,96]{1,2,0:T(8,128)S(1)}, f32[2,326,96]{1,2,0:T(8,128)S(1)}, u32[]{:S(2)}, u32[]{:S(2)}) %collective-permute-start.7) | collective-permute-done | bytes 250400 | tf_op jit(solution)/shard_map/ppermute | solution.py:86
  189.3 2.8 %collective-permute-start.8 = (f32[1,326,96]{1,2,0:T(8,128)S(1)}, f32[1,326,96]{1,2,0:T(8,128)S(1)}, u32[]{:S(2)}, u32[]{:S(2)}) collective-permute-start(f32[1,326,96]{1,2,0:T(8,128)S(1)} %constant_dynamic-slice_fusion), channel_id=1, source_target_pairs={{0,16},{4,20},{8,24},{12,28},{16,0},{20,4},{24,8},{28,12},{1,17},{... | collective-permute-start | bytes 375560 | tf_op jit(solution)/shard_map/ppermute | solution.py:86
  192.1 5.9 %collective-permute-done.8 = f32[1,326,96]{1,2,0:T(8,128)S(1)} collective-permute-done((f32[1,326,96]{1,2,0:T(8,128)S(1)}, f32[1,326,96]{1,2,0:T(8,128)S(1)}, u32[]{:S(2)}, u32[]{:S(2)}) %collective-permute-start.8) | collective-permute-done | bytes 125216 | tf_op jit(solution)/shard_map/ppermute | solution.py:86
  199.6 3.6 %collective-permute-done.9 = f32[326,96]{0,1:T(8,128)S(1)} collective-permute-done((f32[326,96]{0,1:T(8,128)S(1)}, f32[326,96]{0,1:T(8,128)S(1)}, u32[]{:S(2)}, u32[]{:S(2)}) %collective-permute-start.9) | collective-permute-done | bytes 125216 | tf_op jit(solution)/shard_map/ppermute | solution.py:86
  (106 shorter events, 52.4 us)
Async XLA Ops:
  0.6 7.9 %copy-start.1 = (f32[1,4,2,160,96]{4,3,2,1,0:T(8,128)S(1)}, f32[1,4,2,160,96]{4,3,2,1,0:T(8,128)}, u32[]{:S(2)}) copy-start(f32[1,4,2,160,96]{4,3,2,1,0:T(8,128)} %param.13) | copy-start | bytes 1474564
  0.6 10.0 %copy-start.10 = (f32[3,3,3,96,96]{4,3,2,1,0:T(8,128)S(1)}, f32[3,3,3,96,96]{4,3,2,1,0:T(8,128)}, u32[]{:S(2)}) copy-start(f32[3,3,3,96,96]{4,3,2,1,0:T(8,128)} %param.11) | copy-start | bytes 2985988
  3.6 18.9 %collective-permute-start = (f32[1,2,2,160,96]{4,3,2,1,0:T(8,128)S(1)}, f32[1,2,2,160,96]{4,3,2,1,0:T(8,128)S(1)}, u32[]{:S(2)}, u32[]{:S(2)}) collective-permute-start(f32[1,2,2,160,96]{4,3,2,1,0:T(8,128)S(1)} %slice.228), channel_id=1, source_target_pairs={{0,4},{4,8},{8,12},{12,16},{16,20},{20,24},{24,28},{1,5},{5,9},{9,... | collective-permute-start | bytes 737288 | tf_op jit(solution)/shard_map/ppermute | solution.py:12
  9.3 13.9 %collective-permute-start.1 = (f32[1,2,2,160,96]{4,3,2,1,0:T(8,128)}, f32[1,2,2,160,96]{4,3,2,1,0:T(8,128)}, u32[]{:S(2)}, u32[]{:S(2)}) collective-permute-start(f32[1,2,2,160,96]{4,3,2,1,0:T(8,128)} %slice.172), channel_id=1, source_target_pairs={{4,0},{8,4},{12,8},{16,12},{20,16},{24,20},{28,24},{5,1},{9,5},{13... | collective-permute-start | bytes 737288 | tf_op jit(solution)/shard_map/ppermute | solution.py:12
  22.5 0.7 copy-start.11
  25.5 15.8 %collective-permute-start.2 = (f32[2,6,1,160,96]{4,3,2,1,0:T(8,128)}, f32[2,6,1,160,96]{4,3,2,1,0:T(8,128)}, u32[]{:S(2)}, u32[]{:S(2)}) collective-permute-start(f32[2,6,1,160,96]{4,3,2,1,0:T(8,128)} %slice_select_fusion), channel_id=1, source_target_pairs={{0,2},{2,0},{1,3},{3,1},{4,6},{6,4},{5,7},{7,5},{8,10},{10,8},{9,1... | collective-permute-start | bytes 2211848 | tf_op jit(solution)/shard_map/ppermute | solution.py:22
  26.7 5.2 %copy-start.2 = (f32[3,3,3,96,96]{4,3,2,1,0:T(8,128)S(1)}, f32[3,3,3,96,96]{4,3,2,1,0:T(8,128)}, u32[]{:S(2)}) copy-start(f32[3,3,3,96,96]{4,3,2,1,0:T(8,128)} %param.8) | copy-start | bytes 2985988
  55.9 4.2 %copy-start.7 = (f32[864,96]{0,1:T(8,128)S(1)}, f32[864,96]{0,1:T(8,128)}, u32[]{:S(2)}) copy-start(f32[864,96]{0,1:T(8,128)} %copy.67) | copy-start | bytes 995332
  55.9 4.2 %copy-start.8 = (f32[864,96]{0,1:T(8,128)S(1)}, f32[864,96]{0,1:T(8,128)}, u32[]{:S(2)}) copy-start(f32[864,96]{0,1:T(8,128)} %copy.68) | copy-start | bytes 995332
  55.9 4.2 %copy-start.9 = (f32[864,96]{0,1:T(8,128)S(1)}, f32[864,96]{0,1:T(8,128)}, u32[]{:S(2)}) copy-start(f32[864,96]{0,1:T(8,128)} %copy.69) | copy-start | bytes 995332
  60.1 6.2 %copy-start.14 = (f32[96]{0:T(128)S(1)}, f32[96]{0:T(128)}, u32[]{:S(2)}) copy-start(f32[96]{0:T(128)} %param.9) | copy-start | bytes 1156
  67.1 6.8 %copy-start.6 = (f32[864,96]{0,1:T(8,128)S(1)}, f32[864,96]{0,1:T(8,128)}, u32[]{:S(2)}) copy-start(f32[864,96]{0,1:T(8,128)} %copy.64) | copy-start | bytes 995332
  73.9 6.4 %copy-start.13 = (f32[96]{0:T(128)S(1)}, f32[96]{0:T(128)}, u32[]{:S(2)}) copy-start(f32[96]{0:T(128)} %param.12) | copy-start | bytes 1156
  85.7 24.3 %collective-permute-start.3 = (f32[1,2,2,160,96]{4,3,2,1,0:T(8,128)}, f32[1,2,2,160,96]{4,3,2,1,0:T(8,128)}, u32[]{:S(2)}, u32[]{:S(2)}) collective-permute-start(f32[1,2,2,160,96]{4,3,2,1,0:T(8,128)} %slice.242), channel_id=1, source_target_pairs={{4,0},{8,4},{12,8},{16,12},{20,16},{24,20},{28,24},{5,1},{9,5},{13... | collective-permute-start | bytes 737288 | tf_op jit(solution)/shard_map/ppermute | solution.py:12
  111.8 19.2 %collective-permute-start.4 = (f32[1,6,1,160,96]{4,3,2,1,0:T(8,128)}, f32[1,6,1,160,96]{4,3,2,1,0:T(8,128)}, u32[]{:S(2)}, u32[]{:S(2)}) collective-permute-start(f32[1,6,1,160,96]{4,3,2,1,0:T(8,128)} %fusion.38), channel_id=1, source_target_pairs={{0,2},{2,0},{1,3},{3,1},{4,6},{6,4},{5,7},{7,5},{8,10},{10,8},{9,1... | collective-permute-start | bytes 1105928 | tf_op jit(solution)/shard_map/ppermute | solution.py:22
  135.4 6.8 %copy-start.5 = (f32[864,96]{0,1:T(8,128)S(1)}, f32[864,96]{0,1:T(8,128)}, u32[]{:S(2)}) copy-start(f32[864,96]{0,1:T(8,128)} %copy.73) | copy-start | bytes 995332
  142.2 6.7 %copy-start = (f32[1,4,2,160,96]{4,3,2,1,0:T(8,128)S(1)}, f32[1,4,2,160,96]{4,3,2,1,0:T(8,128)}, u32[]{:S(2)}) copy-start(f32[1,4,2,160,96]{4,3,2,1,0:T(8,128)} %param.7) | copy-start | bytes 1474564
  142.2 6.7 %copy-start.12 = (f32[96]{0:T(128)S(1)}, f32[96]{0:T(128)}, u32[]{:S(2)}) copy-start(f32[96]{0:T(128)} %param.10) | copy-start | bytes 1156
  149.9 1.5 copy-start.3
  149.9 1.9 copy-start.4
  159.5 2.9 %collective-permute-start.5 = (f32[1,8,326,96]{2,3,1,0:T(8,128)S(1)}, f32[1,8,326,96]{2,3,1,0:T(8,128)S(1)}, u32[]{:S(2)}, u32[]{:S(2)}) collective-permute-start(f32[1,8,326,96]{2,3,1,0:T(8,128)S(1)} %bitcast.101), channel_id=1, source_target_pairs={{0,2},{2,0},{1,3},{3,1},{4,6},{6,4},{5,7},{7,5},{8,10},{10,8},{9,1... | collective-permute-start | bytes 3004424 | tf_op jit(solution)/shard_map/ppermute | solution.py:86
  162.6 16.8 %collective-permute-start.6 = (f32[4,326,96]{1,2,0:T(8,128)S(1)}, f32[4,326,96]{1,2,0:T(8,128)S(1)}, u32[]{:S(2)}, u32[]{:S(2)}) collective-permute-start(f32[4,326,96]{1,2,0:T(8,128)S(1)} %dynamic-slice_bitcast_fusion), channel_id=1, source_target_pairs={{0,4},{4,0},{8,12},{12,8},{16,20},{20,16},{24,28},{28,24},{1,5},{5... | collective-permute-start | bytes 1502216 | tf_op jit(solution)/shard_map/ppermute | solution.py:86
  179.5 9.7 %collective-permute-start.7 = (f32[2,326,96]{1,2,0:T(8,128)S(1)}, f32[2,326,96]{1,2,0:T(8,128)S(1)}, u32[]{:S(2)}, u32[]{:S(2)}) collective-permute-start(f32[2,326,96]{1,2,0:T(8,128)S(1)} %dynamic-slice_bitcast_fusion.1), channel_id=1, source_target_pairs={{0,8},{4,12},{8,0},{12,4},{16,24},{20,28},{24,16},{28,20},{1,9},{5... | collective-permute-start | bytes 751112 | tf_op jit(solution)/shard_map/ppermute | solution.py:86
  189.3 8.7 %collective-permute-start.8 = (f32[1,326,96]{1,2,0:T(8,128)S(1)}, f32[1,326,96]{1,2,0:T(8,128)S(1)}, u32[]{:S(2)}, u32[]{:S(2)}) collective-permute-start(f32[1,326,96]{1,2,0:T(8,128)S(1)} %constant_dynamic-slice_fusion), channel_id=1, source_target_pairs={{0,16},{4,20},{8,24},{12,28},{16,0},{20,4},{24,8},{28,12},{1,17},{... | collective-permute-start | bytes 375560 | tf_op jit(solution)/shard_map/ppermute | solution.py:86
  198.0 5.2 %collective-permute-start.9 = (f32[326,96]{0,1:T(8,128)S(1)}, f32[326,96]{0,1:T(8,128)S(1)}, u32[]{:S(2)}, u32[]{:S(2)}) collective-permute-start(f32[326,96]{0,1:T(8,128)S(1)} %add_bitcast_fusion), channel_id=1, source_target_pairs={{0,1},{1,0},{2,3},{3,2},{4,5},{5,4},{6,7},{7,6},{8,9},{9,8},{10,11... | collective-permute-start | bytes 375560 | tf_op jit(solution)/shard_map/ppermute | solution.py:86
  203.2 1.4 collective-permute-start.10
where the time goes:
time: 208 us; the launch traced here: 206 us
  local copies, waits for them, and re-layouts  84.8 us (41%)
  waiting for transfers between devices  45.7 us (22%)
  matrix products  32.1 us (15%)
  other arithmetic  23.6 us (11%)
  starting transfers between devices  19.1 us (9%)
    ppermute x6, waiting for transfers between devices, exchanged(): return lax.ppermute(block, axis, [(i, i ^ bit) for i in range(count)])  33.9 us
    concatenate x3, local copies, waits for them, and re-layouts, row_patches(): taps = jnp.concatenate(pieces, axis=-1)  20.6 us
    dot_general x3, matrix products, conv_rows(): out = jnp.dot(taps, stacked, precision=lax.Precision.HIGH)  19.3 us
    ppermute x3, waiting for transfers between devices, passed_along(): return lax.ppermute(block, axis, route)  11.8 us
    ppermute x6, starting transfers between devices, exchanged(): return lax.ppermute(block, axis, [(i, i ^ bit) for i in range(count)])  10.9 us
    another operation x9, local copies, waits for them, and re-layouts, conv_rows(): kernel[:, :, l].reshape(-1, width)  10.4 us
    reshape x2, local copies, waits for them, and re-layouts, row_patches(): return taps.reshape(-1, taps.shape[-1])  8.25 us
    ppermute x3, starting transfers between devices, passed_along(): return lax.ppermute(block, axis, route)  7.67 us
  transfers between devices with their start and end apart: 11, of which 7 were waited for; matrix products, arithmetic and copies ran while one was open for 28% of the time, Pallas kernels for 0%

commit v1 on v0

--- a/solution.py
+++ b/solution.py
@@ -37,11 +37,12 @@
     return jax.nn.silu(values * lax.rsqrt(square + 1e-06) * scales)
 
 
-def row_patches(wide):
+def row_patches(wide, order=(0, 1, 2)):
     frames = wide.shape[1] - 2
     rows = wide.shape[2] - 2
-    edged = jnp.pad(wide, ((0, 0), (0, 0), (0, 0), (1, 1), (0, 0)))
-    pieces = [edged[:, i : i + frames, j : j + rows] for i in range(3) for j in range(3)]
+    extra = -(wide.shape[3] + 2) % 8
+    edged = jnp.pad(wide, ((0, 0), (0, 0), (0, 0), (1, 1 + extra), (0, 0)))
+    pieces = [edged[:, i : i + frames, j : j + rows] for i in order for j in order]
     taps = jnp.concatenate(pieces, axis=-1)
     return taps.reshape(-1, taps.shape[-1])
 
@@ -51,34 +52,37 @@
     width = kernel.shape[-1]
     stacked = jnp.concatenate([kernel[:, :, l].reshape(-1, width) for l in range(3)], axis=1)
     out = jnp.dot(taps, stacked, precision=lax.Precision.HIGH)
-    out = out.reshape(tuple(shape[:3]) + (cols + 2, 3 * width))
+    out = out.reshape(tuple(shape[:3]) + (-1, 3 * width))
     return sum(out[:, :, :, l : l + cols, l * width : (l + 1) * width] for l in range(3))
 
 
-def shifted_columns(values):
+def shifted_columns(values, order=(0, 1, 2)):
+    extra = -(values.shape[3] + 2) % 8
     return jnp.concatenate(
-        [jnp.pad(values, ((0, 0), (0, 0), (0, 0), (l, 2 - l), (0, 0))) for l in range(3)], axis=-1
-    )
-
-
-def kernel_grad_rows(taps, grad):
+        [jnp.pad(values, ((0, 0), (0, 0), (0, 0), (l, 2 - l + extra), (0, 0))) for l in order], axis=-1
+    )
+
+
+def kernel_grad_rows(taps, grad, order=(0, 1, 2)):
     width = grad.shape[-1]
-    flat = lax.optimization_barrier(shifted_columns(grad).reshape(-1, 3 * width).T)
+    flat = lax.optimization_barrier(shifted_columns(grad, order).reshape(-1, 3 * width).T)
     spread = lax.optimization_barrier(jnp.dot(flat, taps, precision=lax.Precision.HIGH))
     spread = spread.reshape(3, width, 3, 3, -1)
+    return spread, width
+
+
+def kernel_grad_forward(taps, grad):
+    spread, width = kernel_grad_rows(taps, grad)
     return jnp.transpose(spread, (2, 3, 0, 4, 1)).reshape(-1, width)
 
 
-def kernel_grad_rows_flipped(values, taps):
-    channels = values.shape[-1]
-    flat = lax.optimization_barrier(shifted_columns(values).reshape(-1, 3 * channels).T)
-    spread = lax.optimization_barrier(jnp.dot(flat, taps, precision=lax.Precision.HIGH))
-    spread = spread.reshape(3, channels, 3, 3, -1)[::-1, :, ::-1, ::-1]
+def kernel_grad_reversed(values, taps):
+    spread, channels = kernel_grad_rows(taps, values, (2, 1, 0))
     return jnp.transpose(spread, (2, 3, 0, 1, 4)).reshape(27 * channels, -1)
 
 
-def flipped(kernel):
-    return jnp.swapaxes(kernel[::-1, ::-1, ::-1], 3, 4)
+def mirrored(kernel):
+    return jnp.swapaxes(kernel[:, :, ::-1], 3, 4)
 
 
 def exchanged(block, axis, bit):
@@ -152,15 +156,15 @@
     acts_taps = row_patches(acts_wide)
     hidden = conv_rows(acts_taps, weight_one, inputs.shape) + bias_one
     gated = norm_act(hidden, gain_two)
-    cot_taps = row_patches(cot_wide)
-    grad_gated = conv_rows(cot_taps, flipped(weight_two), inputs.shape)
-    flat_two = kernel_grad_rows_flipped(gated, cot_taps)
+    cot_taps = row_patches(cot_wide, (2, 1, 0))
+    grad_gated = conv_rows(cot_taps, mirrored(weight_two), inputs.shape)
+    flat_two = kernel_grad_reversed(gated, cot_taps)
     _, pull_norm_two = jax.vjp(norm_act, hidden, gain_two)
     grad_hidden, gain_two_part = pull_norm_two(grad_gated)
     grad_next = passed_along(grad_hidden[:, :2], "tm", -1)
     grad_wide = padded(jnp.concatenate([grad_hidden, grad_next], axis=1), (("height", 2),), 1)
-    grad_acts = conv_rows(row_patches(grad_wide), flipped(weight_one), inputs.shape)
-    flat_one = kernel_grad_rows(acts_taps, grad_hidden)
+    grad_acts = conv_rows(row_patches(grad_wide, (2, 1, 0)), mirrored(weight_one), inputs.shape)
+    flat_one = kernel_grad_forward(acts_taps, grad_hidden)
     _, pull_norm_one = jax.vjp(norm_act, inputs, gain_one)
     grad_part, gain_one_part = pull_norm_one(grad_acts)
     grad_inputs = cotangent + grad_part

time: 208 us -> 185 us (0.89)
  local copies, waits for them, and re-layouts: 84.8 us -> 65.6 us
  other arithmetic: 23.6 us -> 20.9 us
  matrix products: 32.1 us -> 29.9 us
    reshape x5 -> x0, local copies, waits for them, and re-layouts: 13.5 us -> none  [the longest x2 8.25 us: row_patches(): return taps.reshape(-1, taps.shape[-1])]
    rev x1 -> x0, local copies, waits for them, and re-layouts: 6.49 us -> none  [kernel_grad_rows_flipped(): spread = spread.reshape(3, channels, 3, 3, -1)[::-1, :, ::-1, ::-1]]
    dot_general x1 -> x0, matrix products: 5.9 us -> none  [kernel_grad_rows_flipped(): jnp.dot(flat, taps, precision=lax.Precision.HIGH)]
    dot_general x1 -> x2, matrix products: 6.9 us -> 10.7 us  [kernel_grad_rows(): jnp.dot(flat, taps, precision=lax.Precision.HIGH)]
    reshape x1 -> x2, local copies, waits for them, and re-layouts: 2.54 us -> 5.09 us  [kernel_grad_rows(): spread = spread.reshape(3, width, 3, 3, -1)]
  transfers between devices with their start and end apart: 11 -> 11, of which waited for: 7 -> 7; matrix products, arithmetic and copies ran while one was open for 28% -> 22% of each run, Pallas kernels for 0% -> 0%
where the time goes in v1:
time: 185 us; the launch traced here: 183 us
  local copies, waits for them, and re-layouts  65.6 us (35%)
  waiting for transfers between devices  46.5 us (25%)
  matrix products  29.9 us (16%)
  other arithmetic  20.9 us (11%)
  starting transfers between devices  19.3 us (10%)
    ppermute x6, waiting for transfers between devices, exchanged(): return lax.ppermute(block, axis, [(i, i ^ bit) for i in range(count)])  34.3 us
    concatenate x3, local copies, waits for them, and re-layouts, row_patches(): taps = jnp.concatenate(pieces, axis=-1)  20.6 us
    dot_general x3, matrix products, conv_rows(): out = jnp.dot(taps, stacked, precision=lax.Precision.HIGH)  19.1 us
    ppermute x3, waiting for transfers between devices, passed_along(): return lax.ppermute(block, axis, route)  12.1 us
    ppermute x6, starting transfers between devices, exchanged(): return lax.ppermute(block, axis, [(i, i ^ bit) for i in range(count)])  11.4 us
    dot_general x2, matrix products, kernel_grad_rows(): jnp.dot(flat, taps, precision=lax.Precision.HIGH)  10.7 us
    another operation x9, local copies, waits for them, and re-layouts, conv_rows(): kernel[:, :, l].reshape(-1, width)  9.34 us
    ppermute x3, starting transfers between devices, passed_along(): return lax.ppermute(block, axis, route)  7.44 us
  transfers between devices with their start and end apart: 11, of which 7 were waited for; matrix products, arithmetic and copies ran while one was open for 22% of the time, Pallas kernels for 0%

profile of v1, /device:TPU:0, one launch (start us, length us, event | category | flops | bytes accessed | tf_op | source)
XLA Modules:
  0.0 183.4 jit_solution(10201717246452144927)
XLA Ops:
  0.7 1.6 multiply_reduce_fusion.5
  4.4 4.9 %collective-permute-start = (f32[1,2,2,160,96]{4,3,2,1,0:T(8,128)}, f32[1,2,2,160,96]{4,3,2,1,0:T(8,128)S(1)}, u32[]{:S(2)}, u32[]{:S(2)}) collective-permute-start(f32[1,2,2,160,96]{4,3,2,1,0:T(8,128)} %slice.228), channel_id=1, source_target_pairs={{0,4},{4,8},{8,12},{12,16},{16,20},{20,24},{24,28},{1,5},{5,9},{9,... | collective-permute-start | bytes 737288 | tf_op jit(solution)/shard_map/ppermute | solution.py:12
  11.4 12.1 %collective-permute-done = f32[1,2,2,160,96]{4,3,2,1,0:T(8,128)S(1)} collective-permute-done((f32[1,2,2,160,96]{4,3,2,1,0:T(8,128)}, f32[1,2,2,160,96]{4,3,2,1,0:T(8,128)S(1)}, u32[]{:S(2)}, u32[]{:S(2)}) %collective-permute-start) | collective-permute-done | bytes 245792 | tf_op jit(solution)/shard_map/ppermute | solution.py:12
  30.8 1.9 %copy.67 = f32[864,96]{0,1:T(8,128)} copy(f32[864,96]{1,0:T(8,128)} %bitcast.110) | data formatting | bytes 663552 | tf_op jit(solution)/shard_map/reshape;squeeze | solution.py:53
  40.5 4.6 %pad_slice_fusion = (f32[1,4,2,168,96]{4,3,2,1,0:T(8,128)}, f32[1,4,2,168,96]{4,3,2,1,0:T(8,128)}, f32[1,4,2,168,96]{4,3,2,1,0:T(8,128)}, f32[1,4,2,168,96]{4,3,...) fusion(f32[1,6,4,160,96]{4,3,2,1,0:T(8,128)S(1)} %get-tuple-ele, ...), kind=kLoop, calls=%fused_computation.27 | loop fusion | bytes 12238848 | tf_op jit(solution)/shard_map/slice | solution.py:45
  45.1 7.1 %concatenate.57 = f32[1,4,2,168,864]{4,3,2,1,0:T(8,128)} concatenate(f32[1,4,2,168,96]{4,3,2,1,0:T(8,128)} %get-tuple-element.60, f32[1,4,2,168,96]{4,3,2,1,0:T(8,128)} %get-tuple-element.53, f32[1,4,2,168,96]{4,3,2,1,0:T(8,128)} %get-tuple-element.54, f32[1,4,2,168,96]{4,3,2,1,0:T(8,128)} %get-tuple-element.55, f32[1,4,2,168,96]{4,3,2,1,0:T(8,128)} %get-tuple-element.56, ...), dimensions={4} | concatenate | bytes 9289728 | tf_op jit(solution)/shard_map/concatenate | solution.py:46
  52.2 6.2 %fusion.11 = f32[1,4,2,168,288]{4,3,2,1,0:T(8,128)S(1)} fusion(f32[1,4,2,168,864]{4,3,2,1,0:T(8,128)} %concatenate.57, f32[864,96]{0,1:T(8,128)S(1)} %copy-done.11, f32[864,96]{0,1:T(8,128)S(1)} %copy-done.10, f32[864,96]{0,1:T(8,128)S(1)} %copy-done.9), kind=kOutput, calls=%fused_computation.25 | convolution fusion | flops 2007078912 | bytes 7188480 | tf_op jit(solution)/shard_map/dot_general | solution.py:54
  59.7 6.8 %concatenate.55 = f32[1,4,2,168,864]{4,3,2,1,0:T(8,128)} concatenate(f32[1,4,2,168,96]{4,3,2,1,0:T(8,128)S(1)} %copy-done.4, f32[1,4,2,168,96]{4,3,2,1,0:T(8,128)} %get-tuple-element.86, f32[1,4,2,168,96]{4,3,2,1,0:T(8,128)} %get-tuple-element.85, f32[1,4,2,168,96]{4,3,2,1,0:T(8,128)} %get-tuple-element.84, f32[1,4,2,168,96]{4,3,2,1,0:T(8,128)} %get-tuple-element.83, ...), dimensions={4} | concatenate | bytes 9289728 | tf_op jit(solution)/shard_map/concatenate | solution.py:46
  66.6 6.5 %fusion.8 = f32[1,4,2,168,288]{4,3,2,1,0:T(8,128)S(1)} fusion(f32[1,4,2,168,864]{4,3,2,1,0:T(8,128)} %concatenate.55, f32[864,96]{0,1:T(8,128)} %copy.66, f32[864,96]{0,1:T(8,128)} %copy.65, f32[864,96]{0,1:T(8,128)S(1)} %copy-done.8), kind=kOutput, calls=%fused_computation.24 | convolution fusion | flops 2007078912 | bytes 7188480 | tf_op jit(solution)/shard_map/dot_general | solution.py:54
  73.1 1.7 multiply_reduce_fusion
  78.3 4.3 %fusion.55 = f32[288,864]{1,0:T(8,128)} fusion(f32[288,1344]{0,1:T(8,128)S(1)} %bitcast.95, f32[1344,864]{1,0:T(8,128)S(1)} %bitcast.93), kind=kOutput, calls=%fused_computation.127 | convolution fusion | flops 2006581248 | bytes 7188480 | tf_op jit(solution)/shard_map/dot_general | solution.py:69
  82.6 2.5 %reshape.151 = f32[3,96,3,3,96]{4,3,2,1,0:T(4,128)S(1)} reshape(f32[288,864]{1,0:T(8,128)} %fusion.55) | data formatting | bytes 1990656 | tf_op jit(solution)/shard_map/reshape | solution.py:70
  85.1 2.2 %copy.76 = f32[3,3,3,96,96]{4,3,2,1,0:T(8,128)} copy(f32[3,3,3,96,96]{3,1,0,4,2:T(4,128)S(1)} %bitcast.96) | data formatting | bytes 1990656 | tf_op jit(solution)/shard_map/transpose | solution.py:76
  91.1 1.8 %fusion.38 = f32[1,6,1,160,96]{4,3,2,1,0:T(8,128)} fusion(f32[1,4,2,160,96]{4,3,2,1,0:T(8,128)S(1)} %get-tuple-element.25, f32[1,2,2,160,96]{4,3,2,1,0:T(8,128)} %collective-permute-done.3, pred[]{:T(512)S(6)} %eq.13), kind=kLoop, calls=%fused_computation.96 | loop fusion | flops 276480 | bytes 1105921 | tf_op jit(solution)/shard_map/jit(_where)/select_n | solution.py:22
  93.4 6.4 %fusion.56 = f32[288,864]{1,0:T(8,128)} fusion(f32[288,1344]{0,1:T(8,128)S(1)} %bitcast.94, f32[1344,864]{1,0:T(8,128)} %bitcast.90), kind=kOutput, calls=%fused_computation.128 | convolution fusion | flops 2006581248 | bytes 7188480 | tf_op jit(solution)/shard_map/dot_general | solution.py:69
  99.8 2.5 %reshape.154 = f32[3,96,3,3,96]{4,3,2,1,0:T(4,128)S(1)} reshape(f32[288,864]{1,0:T(8,128)} %fusion.56) | data formatting | bytes 1990656 | tf_op jit(solution)/shard_map/reshape | solution.py:70
  105.1 1.5 copy.80
  108.9 2.1 %fusion.49 = (f32[1,4,2,168,96]{4,3,2,1,0:T(8,128)S(1)}, f32[1,4,2,168,96]{4,3,2,1,0:T(8,128)S(1)}, f32[1,4,2,168,96]{4,3,2,1,0:T(8,128)S(1)}, f32[1,4,2,168,96]...) fusion(f32[1,6,4,168,96]{4,3,2,1,0:T(8,128)S(1)} %select_maximu, ...), kind=kLoop, calls=%fused_computation.121 | loop fusion | bytes 9289728 | tf_op jit(solution)/shard_map/slice | solution.py:45
  111.0 6.7 %concatenate.61 = f32[1,4,2,168,864]{4,3,2,1,0:T(8,128)} concatenate(f32[1,4,2,168,96]{4,3,2,1,0:T(8,128)} %get-tuple-element.42, f32[1,4,2,168,96]{4,3,2,1,0:T(8,128)} %get-tuple-element.41, f32[1,4,2,168,96]{4,3,2,1,0:T(8,128)} %get-tuple-element.40, f32[1,4,2,168,96]{4,3,2,1,0:T(8,128)} %get-tuple-element.39, f32[1,4,2,168,96]{4,3,2,1,0:T(8,128)} %get-tuple-element.38, ...), dimensions={4} | concatenate | bytes 9289728 | tf_op jit(solution)/shard_map/concatenate | solution.py:46
  117.7 6.4 %fusion.14 = f32[1,4,2,168,288]{4,3,2,1,0:T(8,128)S(1)} fusion(f32[1,4,2,168,864]{4,3,2,1,0:T(8,128)} %concatenate.61, f32[864,96]{0,1:T(8,128)} %copy.75, f32[864,96]{0,1:T(8,128)} %copy.74, f32[864,96]{0,1:T(8,128)S(1)} %copy-done.7), kind=kOutput, calls=%fused_computation.26 | convolution fusion | flops 2007078912 | bytes 7188480 | tf_op jit(solution)/shard_map/dot_general | solution.py:54
  126.6 3.3 %maximum_multiply_fusion = f32[8,652,96]{1,2,0:T(8,128)} fusion(f32[8,4,96]{1,2,0:T(8,128)S(1)} %broadcast_in_dim.14, f32[8,324,96]{1,2,0:T(8,128)} %copy.80, f32[8,324,96]{1,2,0:T(8,128)S(1)} %copy-done.3), kind=kLoop, calls=%fused_computation.11 | loop fusion | flops 1502208 | bytes 4005888 | tf_op jit(solution)/shard_map/mul | solution.py:201
  129.9 3.3 %mul.209 = f32[8,2,326,96]{2,1,3,0:T(2,128)S(1)} reshape(f32[8,652,96]{1,2,0:T(8,128)} %maximum_multiply_fusion) | data formatting | bytes 4005888 | tf_op jit(solution)/shard_map/mul | solution.py:201
  133.2 2.3 %constant_dynamic-slice_fusion.2 = (f32[8,1,326,96]{2,1,3,0:T(1,128)S(1)}, f32[8,1,326,96]{2,1,3,0:T(1,128)S(1)}) fusion(f32[8,2,326,96]{2,1,3,0:T(2,128)S(1)} %mul.209, s32[]{:T(128)S(6)} %select_n.109, s32[]{:T(128)S(6)} %select_n.110), kind=kLoop, calls=%fused_computation.115 | loop fusion | bytes 4005896 | tf_op jit(solution)/shard_map/dynamic-slice.4
  135.7 2.8 %collective-permute-done.5 = f32[1,8,326,96]{2,3,1,0:T(8,128)S(1)} collective-permute-done((f32[1,8,326,96]{2,3,1,0:T(8,128)S(1)}, f32[1,8,326,96]{2,3,1,0:T(8,128)S(1)}, u32[]{:S(2)}, u32[]{:S(2)}) %collective-permute-start.5) | collective-permute-done | bytes 1001504 | tf_op jit(solution)/shard_map/ppermute | solution.py:90
  138.7 3.1 %collective-permute-start.6 = (f32[4,326,96]{1,2,0:T(8,128)S(1)}, f32[4,326,96]{1,2,0:T(8,128)S(1)}, u32[]{:S(2)}, u32[]{:S(2)}) collective-permute-start(f32[4,326,96]{1,2,0:T(8,128)S(1)} %dynamic-slice_bitcast_fusion), channel_id=1, source_target_pairs={{0,4},{4,0},{8,12},{12,8},{16,20},{20,16},{24,28},{28,24},{1,5},{5... | collective-permute-start | bytes 1502216 | tf_op jit(solution)/shard_map/ppermute | solution.py:90
  141.8 13.6 %collective-permute-done.6 = f32[4,326,96]{1,2,0:T(8,128)S(1)} collective-permute-done((f32[4,326,96]{1,2,0:T(8,128)S(1)}, f32[4,326,96]{1,2,0:T(8,128)S(1)}, u32[]{:S(2)}, u32[]{:S(2)}) %collective-permute-start.6) | collective-permute-done | bytes 500768 | tf_op jit(solution)/shard_map/ppermute | solution.py:90
  155.5 3.1 %collective-permute-start.7 = (f32[2,326,96]{1,2,0:T(8,128)S(1)}, f32[2,326,96]{1,2,0:T(8,128)S(1)}, u32[]{:S(2)}, u32[]{:S(2)}) collective-permute-start(f32[2,326,96]{1,2,0:T(8,128)S(1)} %dynamic-slice_bitcast_fusion.1), channel_id=1, source_target_pairs={{0,8},{4,12},{8,0},{12,4},{16,24},{20,28},{24,16},{28,20},{1,9},{5... | collective-permute-start | bytes 751112 | tf_op jit(solution)/shard_map/ppermute | solution.py:90
  158.6 6.6 %collective-permute-done.7 = f32[2,326,96]{1,2,0:T(8,128)S(1)} collective-permute-done((f32[2,326,96]{1,2,0:T(8,128)S(1)}, f32[2,326,96]{1,2,0:T(8,128)S(1)}, u32[]{:S(2)}, u32[]{:S(2)}) %collective-permute-start.7) | collective-permute-done | bytes 250400 | tf_op jit(solution)/shard_map/ppermute | solution.py:90
  165.3 3.5 %collective-permute-start.8 = (f32[1,326,96]{1,2,0:T(8,128)S(1)}, f32[1,326,96]{1,2,0:T(8,128)S(1)}, u32[]{:S(2)}, u32[]{:S(2)}) collective-permute-start(f32[1,326,96]{1,2,0:T(8,128)S(1)} %constant_dynamic-slice_fusion), channel_id=1, source_target_pairs={{0,16},{4,20},{8,24},{12,28},{16,0},{20,4},{24,8},{28,12},{1,17},{... | collective-permute-start | bytes 375560 | tf_op jit(solution)/shard_map/ppermute | solution.py:90
  168.7 6.3 %collective-permute-done.8 = f32[1,326,96]{1,2,0:T(8,128)S(1)} collective-permute-done((f32[1,326,96]{1,2,0:T(8,128)S(1)}, f32[1,326,96]{1,2,0:T(8,128)S(1)}, u32[]{:S(2)}, u32[]{:S(2)}) %collective-permute-start.8) | collective-permute-done | bytes 125216 | tf_op jit(solution)/shard_map/ppermute | solution.py:90
  175.1 1.6 collective-permute-start.9
  176.7 3.6 %collective-permute-done.9 = f32[326,96]{0,1:T(8,128)S(1)} collective-permute-done((f32[326,96]{0,1:T(8,128)S(1)}, f32[326,96]{0,1:T(8,128)S(1)}, u32[]{:S(2)}, u32[]{:S(2)}) %collective-permute-start.9) | collective-permute-done | bytes 125216 | tf_op jit(solution)/shard_map/ppermute | solution.py:90
  (116 shorter events, 39.1 us)
Async XLA Ops:
  0.6 8.6 %copy-start.1 = (f32[1,4,2,160,96]{4,3,2,1,0:T(8,128)S(1)}, f32[1,4,2,160,96]{4,3,2,1,0:T(8,128)}, u32[]{:S(2)}) copy-start(f32[1,4,2,160,96]{4,3,2,1,0:T(8,128)} %param.13) | copy-start | bytes 1474564
  0.6 10.7 %copy-start.12 = (f32[3,3,3,96,96]{4,3,2,1,0:T(8,128)S(1)}, f32[3,3,3,96,96]{4,3,2,1,0:T(8,128)}, u32[]{:S(2)}) copy-start(f32[3,3,3,96,96]{4,3,2,1,0:T(8,128)} %param.11) | copy-start | bytes 2985988
  4.4 19.2 %collective-permute-start = (f32[1,2,2,160,96]{4,3,2,1,0:T(8,128)}, f32[1,2,2,160,96]{4,3,2,1,0:T(8,128)S(1)}, u32[]{:S(2)}, u32[]{:S(2)}) collective-permute-start(f32[1,2,2,160,96]{4,3,2,1,0:T(8,128)} %slice.228), channel_id=1, source_target_pairs={{0,4},{4,8},{8,12},{12,16},{16,20},{20,24},{24,28},{1,5},{5,9},{9,... | collective-permute-start | bytes 737288 | tf_op jit(solution)/shard_map/ppermute | solution.py:12
  10.0 13.5 %collective-permute-start.1 = (f32[1,2,2,160,96]{4,3,2,1,0:T(8,128)}, f32[1,2,2,160,96]{4,3,2,1,0:T(8,128)S(1)}, u32[]{:S(2)}, u32[]{:S(2)}) collective-permute-start(f32[1,2,2,160,96]{4,3,2,1,0:T(8,128)} %slice.172), channel_id=1, source_target_pairs={{4,0},{8,4},{12,8},{16,12},{20,16},{24,20},{28,24},{5,1},{9,5},{13... | collective-permute-start | bytes 737288 | tf_op jit(solution)/shard_map/ppermute | solution.py:12
  23.5 1.2 copy-start.13
  23.5 1.2 copy-start.15
  24.8 13.4 %collective-permute-start.2 = (f32[2,6,1,160,96]{4,3,2,1,0:T(8,128)}, f32[2,6,1,160,96]{4,3,2,1,0:T(8,128)}, u32[]{:S(2)}, u32[]{:S(2)}) collective-permute-start(f32[2,6,1,160,96]{4,3,2,1,0:T(8,128)} %slice_select_fusion), channel_id=1, source_target_pairs={{0,2},{2,0},{1,3},{3,1},{4,6},{6,4},{5,7},{7,5},{8,10},{10,8},{9,1... | collective-permute-start | bytes 2211848 | tf_op jit(solution)/shard_map/ppermute | solution.py:22
  25.8 4.2 %copy-start.2 = (f32[3,3,3,96,96]{4,3,2,1,0:T(8,128)S(1)}, f32[3,3,3,96,96]{4,3,2,1,0:T(8,128)}, u32[]{:S(2)}) copy-start(f32[3,3,3,96,96]{4,3,2,1,0:T(8,128)} %param.8) | copy-start | bytes 2985988
  37.2 2.4 %copy-start.14 = (f32[1,2,2,160,96]{4,3,2,1,0:T(8,128)S(1)}, f32[1,2,2,160,96]{4,3,2,1,0:T(8,128)}, u32[]{:S(2)}) copy-start(f32[1,2,2,160,96]{4,3,2,1,0:T(8,128)} %copy-done.13) | copy-start | bytes 737284
  37.3 2.4 %copy-start.16 = (f32[1,2,2,160,96]{4,3,2,1,0:T(8,128)S(1)}, f32[1,2,2,160,96]{4,3,2,1,0:T(8,128)}, u32[]{:S(2)}) copy-start(f32[1,2,2,160,96]{4,3,2,1,0:T(8,128)} %copy-done.15) | copy-start | bytes 737284
  45.1 7.1 %copy-start.9 = (f32[864,96]{0,1:T(8,128)S(1)}, f32[864,96]{0,1:T(8,128)}, u32[]{:S(2)}) copy-start(f32[864,96]{0,1:T(8,128)} %copy.67) | copy-start | bytes 995332
  45.1 7.1 %copy-start.10 = (f32[864,96]{0,1:T(8,128)S(1)}, f32[864,96]{0,1:T(8,128)}, u32[]{:S(2)}) copy-start(f32[864,96]{0,1:T(8,128)} %copy.68) | copy-start | bytes 995332
  45.1 7.1 %copy-start.11 = (f32[864,96]{0,1:T(8,128)S(1)}, f32[864,96]{0,1:T(8,128)}, u32[]{:S(2)}) copy-start(f32[864,96]{0,1:T(8,128)} %copy.69) | copy-start | bytes 995332
  52.2 6.2 %copy-start.19 = (f32[96]{0:T(128)S(1)}, f32[96]{0:T(128)}, u32[]{:S(2)}) copy-start(f32[96]{0:T(128)} %param.9) | copy-start | bytes 1156
  58.4 1.3 copy-start.5
  59.7 6.8 %copy-start.8 = (f32[864,96]{0,1:T(8,128)S(1)}, f32[864,96]{0,1:T(8,128)}, u32[]{:S(2)}) copy-start(f32[864,96]{0,1:T(8,128)} %copy.64) | copy-start | bytes 995332
  66.6 6.5 %copy-start.18 = (f32[96]{0:T(128)S(1)}, f32[96]{0:T(128)}, u32[]{:S(2)}) copy-start(f32[96]{0:T(128)} %param.12) | copy-start | bytes 1156
  66.6 11.7 %slice-start = ((s8[4816896]{0:T(1024)(128)(4,1)}), s8[4194304]{0:T(1024)(128)(4,1)S(1)}, s32[]{:S(2)}) async-start(s8[4816896]{0:T(1024)(128)(4,1)} %bitcast.91), calls=%async_computation | async-start | bytes 8388608
  73.1 5.2 %slice-start.1 = ((s8[4816896]{0:T(1024)(128)(4,1)}), s8[622592]{0:T(1024)(128)(4,1)S(1)}, s32[]{:S(2)}) async-start(s8[4816896]{0:T(1024)(128)(4,1)} %bitcast.91), calls=%async_computation.1 | async-start | bytes 1245184
  77.0 14.1 %collective-permute-start.3 = (f32[1,2,2,160,96]{4,3,2,1,0:T(8,128)}, f32[1,2,2,160,96]{4,3,2,1,0:T(8,128)}, u32[]{:S(2)}, u32[]{:S(2)}) collective-permute-start(f32[1,2,2,160,96]{4,3,2,1,0:T(8,128)} %slice.242), channel_id=1, source_target_pairs={{4,0},{8,4},{12,8},{16,12},{20,16},{24,20},{28,24},{5,1},{9,5},{13... | collective-permute-start | bytes 737288 | tf_op jit(solution)/shard_map/ppermute | solution.py:12
  87.3 3.0 %copy-start.6 = (f32[1,4,2,160,96]{4,3,2,1,0:T(8,128)S(1)}, f32[1,4,2,160,96]{4,3,2,1,0:T(8,128)}, u32[]{:S(2)}) copy-start(f32[1,4,2,160,96]{4,3,2,1,0:T(8,128)} %get-tuple-element.72) | copy-start | bytes 1474564
  92.9 13.7 %collective-permute-start.4 = (f32[1,6,1,160,96]{4,3,2,1,0:T(8,128)}, f32[1,6,1,160,96]{4,3,2,1,0:T(8,128)}, u32[]{:S(2)}, u32[]{:S(2)}) collective-permute-start(f32[1,6,1,160,96]{4,3,2,1,0:T(8,128)} %fusion.38), channel_id=1, source_target_pairs={{0,2},{2,0},{1,3},{3,1},{4,6},{6,4},{5,7},{7,5},{8,10},{10,8},{9,1... | collective-permute-start | bytes 1105928 | tf_op jit(solution)/shard_map/ppermute | solution.py:22
  111.0 6.7 %copy-start.7 = (f32[864,96]{0,1:T(8,128)S(1)}, f32[864,96]{0,1:T(8,128)}, u32[]{:S(2)}) copy-start(f32[864,96]{0,1:T(8,128)} %copy.73) | copy-start | bytes 995332
  117.7 6.5 %copy-start = (f32[1,4,2,160,96]{4,3,2,1,0:T(8,128)S(1)}, f32[1,4,2,160,96]{4,3,2,1,0:T(8,128)}, u32[]{:S(2)}) copy-start(f32[1,4,2,160,96]{4,3,2,1,0:T(8,128)} %param.7) | copy-start | bytes 1474564
  117.7 6.5 %copy-start.17 = (f32[96]{0:T(128)S(1)}, f32[96]{0:T(128)}, u32[]{:S(2)}) copy-start(f32[96]{0:T(128)} %param.10) | copy-start | bytes 1156
  125.1 1.4 copy-start.3
  135.6 2.9 %collective-permute-start.5 = (f32[1,8,326,96]{2,3,1,0:T(8,128)S(1)}, f32[1,8,326,96]{2,3,1,0:T(8,128)S(1)}, u32[]{:S(2)}, u32[]{:S(2)}) collective-permute-start(f32[1,8,326,96]{2,3,1,0:T(8,128)S(1)} %bitcast.111), channel_id=1, source_target_pairs={{0,2},{2,0},{1,3},{3,1},{4,6},{6,4},{5,7},{7,5},{8,10},{10,8},{9,1... | collective-permute-start | bytes 3004424 | tf_op jit(solution)/shard_map/ppermute | solution.py:90
  138.7 16.7 %collective-permute-start.6 = (f32[4,326,96]{1,2,0:T(8,128)S(1)}, f32[4,326,96]{1,2,0:T(8,128)S(1)}, u32[]{:S(2)}, u32[]{:S(2)}) collective-permute-start(f32[4,326,96]{1,2,0:T(8,128)S(1)} %dynamic-slice_bitcast_fusion), channel_id=1, source_target_pairs={{0,4},{4,0},{8,12},{12,8},{16,20},{20,16},{24,28},{28,24},{1,5},{5... | collective-permute-start | bytes 1502216 | tf_op jit(solution)/shard_map/ppermute | solution.py:90
  155.5 9.7 %collective-permute-start.7 = (f32[2,326,96]{1,2,0:T(8,128)S(1)}, f32[2,326,96]{1,2,0:T(8,128)S(1)}, u32[]{:S(2)}, u32[]{:S(2)}) collective-permute-start(f32[2,326,96]{1,2,0:T(8,128)S(1)} %dynamic-slice_bitcast_fusion.1), channel_id=1, source_target_pairs={{0,8},{4,12},{8,0},{12,4},{16,24},{20,28},{24,16},{28,20},{1,9},{5... | collective-permute-start | bytes 751112 | tf_op jit(solution)/shard_map/ppermute | solution.py:90
  165.3 9.8 %collective-permute-start.8 = (f32[1,326,96]{1,2,0:T(8,128)S(1)}, f32[1,326,96]{1,2,0:T(8,128)S(1)}, u32[]{:S(2)}, u32[]{:S(2)}) collective-permute-start(f32[1,326,96]{1,2,0:T(8,128)S(1)} %constant_dynamic-slice_fusion), channel_id=1, source_target_pairs={{0,16},{4,20},{8,24},{12,28},{16,0},{20,4},{24,8},{28,12},{1,17},{... | collective-permute-start | bytes 375560 | tf_op jit(solution)/shard_map/ppermute | solution.py:90
  175.1 5.2 %collective-permute-start.9 = (f32[326,96]{0,1:T(8,128)S(1)}, f32[326,96]{0,1:T(8,128)S(1)}, u32[]{:S(2)}, u32[]{:S(2)}) collective-permute-start(f32[326,96]{0,1:T(8,128)S(1)} %add_bitcast_fusion), channel_id=1, source_target_pairs={{0,1},{1,0},{2,3},{3,2},{4,5},{5,4},{6,7},{7,6},{8,9},{9,8},{10,11... | collective-permute-start | bytes 375560 | tf_op jit(solution)/shard_map/ppermute | solution.py:90
  180.3 1.4 collective-permute-start.10
  (1 other events, 1.1 us)

commit v2 on v1

--- a/solution.py
+++ b/solution.py
@@ -50,7 +50,7 @@
 def conv_rows(taps, kernel, shape):
     cols = shape[3]
     width = kernel.shape[-1]
-    stacked = jnp.concatenate([kernel[:, :, l].reshape(-1, width) for l in range(3)], axis=1)
+    stacked = jnp.transpose(kernel, (0, 1, 3, 2, 4)).reshape(-1, 3 * width)
     out = jnp.dot(taps, stacked, precision=lax.Precision.HIGH)
     out = out.reshape(tuple(shape[:3]) + (-1, 3 * width))
     return sum(out[:, :, :, l : l + cols, l * width : (l + 1) * width] for l in range(3))

time: 185 us -> 183 us (0.989)
  local copies, waits for them, and re-layouts: 65.6 us -> 63.1 us
    another operation x10 -> x5, local copies, waits for them, and re-layouts: 11.6 us -> 5.6 us  [the longest x4 3.32 us: conv_rows(): stacked = jnp.transpose(kernel, (0, 1, 3, 2, 4)).reshape(-1, 3 * width)]
    reshape x0 -> x3, local copies, waits for them, and re-layouts: none -> 4.87 us  [conv_rows(): stacked = jnp.transpose(kernel, (0, 1, 3, 2, 4)).reshape(-1, 3 * width)]
    slice x9 -> x0, local copies, waits for them, and re-layouts: 3.92 us -> none  [conv_rows(): kernel[:, :, l].reshape(-1, width)]
    transpose x2 -> x1, local copies, waits for them, and re-layouts: 0.17 us -> 2.6 us  [conv_rows(): stacked = jnp.transpose(kernel, (0, 1, 3, 2, 4)).reshape(-1, 3 * width)]
  transfers between devices with their start and end apart: 11 -> 11, of which waited for: 7 -> 7; matrix products, arithmetic and copies ran while one was open for 22% -> 20% of each run, Pallas kernels for 0% -> 0%
where the time goes in v2:
time: 183 us; the launch traced here: 181 us
  local copies, waits for them, and re-layouts  63.1 us (34%)
  waiting for transfers between devices  47 us (26%)
  matrix products  29.7 us (16%)
  other arithmetic  20.7 us (11%)
  starting transfers between devices  19.6 us (11%)
    ppermute x6, waiting for transfers between devices, exchanged(): return lax.ppermute(block, axis, [(i, i ^ bit) for i in range(count)])  34.4 us
    concatenate x3, local copies, waits for them, and re-layouts, row_patches(): taps = jnp.concatenate(pieces, axis=-1)  21.1 us
    dot_general x3, matrix products, conv_rows(): out = jnp.dot(taps, stacked, precision=lax.Precision.HIGH)  19 us
    ppermute x3, waiting for transfers between devices, passed_along(): return lax.ppermute(block, axis, route)  12.6 us
    ppermute x6, starting transfers between devices, exchanged(): return lax.ppermute(block, axis, [(i, i ^ bit) for i in range(count)])  12.1 us
    dot_general x2, matrix products, kernel_grad_rows(): jnp.dot(flat, taps, precision=lax.Precision.HIGH)  10.7 us
    ppermute x3, starting transfers between devices, passed_along(): return lax.ppermute(block, axis, route)  7.46 us
    slice x2, local copies, waits for them, and re-layouts, row_patches(): pieces = [edged[:, i:i + frames, j:j + rows] for i in order for j in order]  6.97 us
  transfers between devices with their start and end apart: 11, of which 7 were waited for; matrix products, arithmetic and copies ran while one was open for 20% of the time, Pallas kernels for 0%

profile of v2, /device:TPU:0, one launch (start us, length us, event | category | flops | bytes accessed | tf_op | source)
XLA Modules:
  0.0 181.3 jit_solution(10690051032919757094)
XLA Ops:
  3.6 4.9 %collective-permute-start = (f32[1,2,2,160,96]{4,3,2,1,0:T(8,128)S(1)}, f32[1,2,2,160,96]{4,3,2,1,0:T(8,128)S(1)}, u32[]{:S(2)}, u32[]{:S(2)}) collective-permute-start(f32[1,2,2,160,96]{4,3,2,1,0:T(8,128)S(1)} %slice.192), channel_id=1, source_target_pairs={{0,4},{4,8},{8,12},{12,16},{16,20},{20,24},{24,28},{1,5},{5,9},{9,... | collective-permute-start | bytes 737288 | tf_op jit(solution)/shard_map/ppermute | solution.py:12
  9.8 12.6 %collective-permute-done = f32[1,2,2,160,96]{4,3,2,1,0:T(8,128)S(1)} collective-permute-done((f32[1,2,2,160,96]{4,3,2,1,0:T(8,128)S(1)}, f32[1,2,2,160,96]{4,3,2,1,0:T(8,128)S(1)}, u32[]{:S(2)}, u32[]{:S(2)}) %collective-permute-start) | collective-permute-done | bytes 245792 | tf_op jit(solution)/shard_map/ppermute | solution.py:12
  26.0 1.6 reshape.168
  27.6 2.6 %copy.29 = f32[3,3,96,3,96]{2,1,0,4,3:T(4,128)S(1)} copy(f32[3,3,96,3,96]{4,2,3,1,0:T(8,128)} %bitcast.90) | data formatting | bytes 1990656 | tf_op jit(solution)/shard_map/transpose | solution.py:53
  30.2 1.6 reshape.169
  34.2 1.6 reshape.170
  37.9 4.5 %pad_slice_fusion = (f32[1,4,2,168,96]{4,3,2,1,0:T(8,128)}, f32[1,4,2,168,96]{4,3,2,1,0:T(8,128)}, f32[1,4,2,168,96]{4,3,2,1,0:T(8,128)}, f32[1,4,2,168,96]{4,3,...) fusion(f32[1,6,4,160,96]{4,3,2,1,0:T(8,128)S(1)} %get-tuple-ele, ...), kind=kLoop, calls=%fused_computation.27 | loop fusion | bytes 12238848 | tf_op jit(solution)/shard_map/slice | solution.py:45
  42.5 7.1 %concatenate.47 = f32[1,4,2,168,864]{4,3,2,1,0:T(8,128)} concatenate(f32[1,4,2,168,96]{4,3,2,1,0:T(8,128)} %get-tuple-element.60, f32[1,4,2,168,96]{4,3,2,1,0:T(8,128)} %get-tuple-element.53, f32[1,4,2,168,96]{4,3,2,1,0:T(8,128)} %get-tuple-element.54, f32[1,4,2,168,96]{4,3,2,1,0:T(8,128)} %get-tuple-element.55, f32[1,4,2,168,96]{4,3,2,1,0:T(8,128)} %get-tuple-element.56, ...), dimensions={4} | concatenate | bytes 9289728 | tf_op jit(solution)/shard_map/concatenate | solution.py:46
  49.5 6.2 %fusion.11 = f32[1,4,2,168,288]{4,3,2,1,0:T(8,128)S(1)} fusion(f32[1,4,2,168,864]{4,3,2,1,0:T(8,128)} %concatenate.47, f32[864,288,1,1]{0,1,2,3:T(8,128)S(1)} %copy-done.5), kind=kOutput, calls=%fused_computation.25 | convolution fusion | flops 2006581248 | bytes 7188480 | tf_op jit(solution)/shard_map/dot_general | solution.py:54
  56.5 7.1 %concatenate.46 = f32[1,4,2,168,864]{4,3,2,1,0:T(8,128)} concatenate(f32[1,4,2,168,96]{4,3,2,1,0:T(8,128)} %get-tuple-element.70, f32[1,4,2,168,96]{4,3,2,1,0:T(8,128)} %get-tuple-element.77, f32[1,4,2,168,96]{4,3,2,1,0:T(8,128)} %get-tuple-element.76, f32[1,4,2,168,96]{4,3,2,1,0:T(8,128)} %get-tuple-element.75, f32[1,4,2,168,96]{4,3,2,1,0:T(8,128)} %get-tuple-element.74, ...), dimensions={4} | concatenate | bytes 9289728 | tf_op jit(solution)/shard_map/concatenate | solution.py:46
  63.6 6.5 %fusion.8 = f32[1,4,2,168,288]{4,3,2,1,0:T(8,128)S(1)} fusion(f32[1,4,2,168,864]{4,3,2,1,0:T(8,128)} %concatenate.46, f32[864,288,1,1]{0,1,2,3:T(8,128)S(1)} %copy-done.4), kind=kOutput, calls=%fused_computation.24 | convolution fusion | flops 2006581248 | bytes 7188480 | tf_op jit(solution)/shard_map/dot_general | solution.py:54
  70.2 1.7 multiply_reduce_fusion
  75.4 4.3 %fusion.40 = f32[288,864]{1,0:T(8,128)} fusion(f32[288,1344]{0,1:T(8,128)S(1)} %bitcast.87, f32[1344,864]{1,0:T(8,128)S(1)} %bitcast.85), kind=kOutput, calls=%fused_computation.109 | convolution fusion | flops 2006581248 | bytes 7188480 | tf_op jit(solution)/shard_map/dot_general | solution.py:69
  79.6 2.5 %reshape.163 = f32[3,96,3,3,96]{4,3,2,1,0:T(4,128)S(1)} reshape(f32[288,864]{1,0:T(8,128)} %fusion.40) | data formatting | bytes 1990656 | tf_op jit(solution)/shard_map/reshape | solution.py:70
  82.2 2.2 %copy.31 = f32[3,3,3,96,96]{4,3,2,1,0:T(8,128)} copy(f32[3,3,3,96,96]{3,1,0,4,2:T(4,128)S(1)} %bitcast.88) | data formatting | bytes 1990656 | tf_op jit(solution)/shard_map/transpose | solution.py:76
  88.2 1.8 %fusion.29 = f32[1,6,1,160,96]{4,3,2,1,0:T(8,128)} fusion(f32[1,4,2,160,96]{4,3,2,1,0:T(8,128)S(1)} %get-tuple-element.25, f32[1,2,2,160,96]{4,3,2,1,0:T(8,128)} %collective-permute-done.3, pred[]{:T(512)S(6)} %eq.13), kind=kLoop, calls=%fused_computation.84 | loop fusion | flops 276480 | bytes 1105921 | tf_op jit(solution)/shard_map/jit(_where)/select_n | solution.py:22
  90.0 6.4 %fusion.41 = f32[288,864]{1,0:T(8,128)} fusion(f32[288,1344]{0,1:T(8,128)S(1)} %bitcast.86, f32[1344,864]{1,0:T(8,128)} %bitcast.82), kind=kOutput, calls=%fused_computation.110 | convolution fusion | flops 2006581248 | bytes 7188480 | tf_op jit(solution)/shard_map/dot_general | solution.py:69
  96.4 2.5 %reshape.166 = f32[3,96,3,3,96]{4,3,2,1,0:T(4,128)S(1)} reshape(f32[288,864]{1,0:T(8,128)} %fusion.41) | data formatting | bytes 1990656 | tf_op jit(solution)/shard_map/reshape | solution.py:70
  105.4 2.5 %fusion.37 = (f32[1,4,2,168,96]{4,3,2,1,0:T(8,128)S(1)}, f32[1,4,2,168,96]{4,3,2,1,0:T(8,128)}, f32[1,4,2,168,96]{4,3,2,1,0:T(8,128)}, f32[1,4,2,168,96]{4,3,2,1...) fusion(f32[1,6,4,168,96]{4,3,2,1,0:T(8,128)S(1)} %select_maximu, ...), kind=kLoop, calls=%fused_computation.106 | loop fusion | bytes 9289728 | tf_op jit(solution)/shard_map/slice | solution.py:45
  107.9 7.0 %concatenate.50 = f32[1,4,2,168,864]{4,3,2,1,0:T(8,128)} concatenate(f32[1,4,2,168,96]{4,3,2,1,0:T(8,128)} %get-tuple-element.42, f32[1,4,2,168,96]{4,3,2,1,0:T(8,128)} %get-tuple-element.41, f32[1,4,2,168,96]{4,3,2,1,0:T(8,128)} %get-tuple-element.40, f32[1,4,2,168,96]{4,3,2,1,0:T(8,128)} %get-tuple-element.39, f32[1,4,2,168,96]{4,3,2,1,0:T(8,128)} %get-tuple-element.38, ...), dimensions={4} | concatenate | bytes 9289728 | tf_op jit(solution)/shard_map/concatenate | solution.py:46
  115.0 6.3 %fusion.14 = f32[1,4,2,168,288]{4,3,2,1,0:T(8,128)S(1)} fusion(f32[1,4,2,168,864]{4,3,2,1,0:T(8,128)} %concatenate.50, f32[864,288,1,1]{0,1,2,3:T(8,128)S(1)} %copy-done.3), kind=kOutput, calls=%fused_computation.26 | convolution fusion | flops 2006581248 | bytes 7188480 | tf_op jit(solution)/shard_map/dot_general | solution.py:54
  123.7 3.3 %maximum_multiply_fusion = f32[8,652,96]{1,2,0:T(8,128)} fusion(f32[8,4,96]{1,2,0:T(8,128)S(1)} %broadcast_in_dim.14, f32[8,324,96]{1,2,0:T(8,128)} %copy.35, f32[8,324,96]{1,2,0:T(8,128)S(1)} %copy-done.2), kind=kLoop, calls=%fused_computation.11 | loop fusion | flops 1502208 | bytes 4005888 | tf_op jit(solution)/shard_map/mul | solution.py:201
  127.0 3.3 %mul.209 = f32[8,2,326,96]{2,1,3,0:T(2,128)S(1)} reshape(f32[8,652,96]{1,2,0:T(8,128)} %maximum_multiply_fusion) | data formatting | bytes 4005888 | tf_op jit(solution)/shard_map/mul | solution.py:201
  130.3 2.3 %constant_dynamic-slice_fusion.2 = (f32[8,1,326,96]{2,1,3,0:T(1,128)S(1)}, f32[8,1,326,96]{2,1,3,0:T(1,128)S(1)}) fusion(f32[8,2,326,96]{2,1,3,0:T(2,128)S(1)} %mul.209, s32[]{:T(128)S(6)} %select_n.109, s32[]{:T(128)S(6)} %select_n.110), kind=kLoop, calls=%fused_computation.103 | loop fusion | bytes 4005896 | tf_op jit(solution)/shard_map/dynamic-slice.4
  133.2 2.5 %collective-permute-done.5 = f32[1,8,326,96]{2,3,1,0:T(8,128)S(1)} collective-permute-done((f32[1,8,326,96]{2,3,1,0:T(8,128)S(1)}, f32[1,8,326,96]{2,3,1,0:T(8,128)S(1)}, u32[]{:S(2)}, u32[]{:S(2)}) %collective-permute-start.5) | collective-permute-done | bytes 1001504 | tf_op jit(solution)/shard_map/ppermute | solution.py:90
  135.9 3.2 %collective-permute-start.6 = (f32[4,326,96]{1,2,0:T(8,128)S(1)}, f32[4,326,96]{1,2,0:T(8,128)S(1)}, u32[]{:S(2)}, u32[]{:S(2)}) collective-permute-start(f32[4,326,96]{1,2,0:T(8,128)S(1)} %dynamic-slice_bitcast_fusion), channel_id=1, source_target_pairs={{0,4},{4,0},{8,12},{12,8},{16,20},{20,16},{24,28},{28,24},{1,5},{5... | collective-permute-start | bytes 1502216 | tf_op jit(solution)/shard_map/ppermute | solution.py:90
  139.1 13.9 %collective-permute-done.6 = f32[4,326,96]{1,2,0:T(8,128)S(1)} collective-permute-done((f32[4,326,96]{1,2,0:T(8,128)S(1)}, f32[4,326,96]{1,2,0:T(8,128)S(1)}, u32[]{:S(2)}, u32[]{:S(2)}) %collective-permute-start.6) | collective-permute-done | bytes 500768 | tf_op jit(solution)/shard_map/ppermute | solution.py:90
  153.0 3.3 %collective-permute-start.7 = (f32[2,326,96]{1,2,0:T(8,128)S(1)}, f32[2,326,96]{1,2,0:T(8,128)S(1)}, u32[]{:S(2)}, u32[]{:S(2)}) collective-permute-start(f32[2,326,96]{1,2,0:T(8,128)S(1)} %dynamic-slice_bitcast_fusion.1), channel_id=1, source_target_pairs={{0,8},{4,12},{8,0},{12,4},{16,24},{20,28},{24,16},{28,20},{1,9},{5... | collective-permute-start | bytes 751112 | tf_op jit(solution)/shard_map/ppermute | solution.py:90
  156.3 6.7 %collective-permute-done.7 = f32[2,326,96]{1,2,0:T(8,128)S(1)} collective-permute-done((f32[2,326,96]{1,2,0:T(8,128)S(1)}, f32[2,326,96]{1,2,0:T(8,128)S(1)}, u32[]{:S(2)}, u32[]{:S(2)}) %collective-permute-start.7) | collective-permute-done | bytes 250400 | tf_op jit(solution)/shard_map/ppermute | solution.py:90
  163.1 3.5 %collective-permute-start.8 = (f32[1,326,96]{1,2,0:T(8,128)S(1)}, f32[1,326,96]{1,2,0:T(8,128)S(1)}, u32[]{:S(2)}, u32[]{:S(2)}) collective-permute-start(f32[1,326,96]{1,2,0:T(8,128)S(1)} %constant_dynamic-slice_fusion), channel_id=1, source_target_pairs={{0,16},{4,20},{8,24},{12,28},{16,0},{20,4},{24,8},{28,12},{1,17},{... | collective-permute-start | bytes 375560 | tf_op jit(solution)/shard_map/ppermute | solution.py:90
  166.5 6.4 %collective-permute-done.8 = f32[1,326,96]{1,2,0:T(8,128)S(1)} collective-permute-done((f32[1,326,96]{1,2,0:T(8,128)S(1)}, f32[1,326,96]{1,2,0:T(8,128)S(1)}, u32[]{:S(2)}, u32[]{:S(2)}) %collective-permute-start.8) | collective-permute-done | bytes 125216 | tf_op jit(solution)/shard_map/ppermute | solution.py:90
  174.5 3.6 %collective-permute-done.9 = f32[326,96]{0,1:T(8,128)S(1)} collective-permute-done((f32[326,96]{0,1:T(8,128)S(1)}, f32[326,96]{0,1:T(8,128)S(1)}, u32[]{:S(2)}, u32[]{:S(2)}) %collective-permute-start.9) | collective-permute-done | bytes 125216 | tf_op jit(solution)/shard_map/ppermute | solution.py:90
  (90 shorter events, 34.7 us)
Async XLA Ops:
  0.6 7.8 %copy-start.1 = (f32[1,4,2,160,96]{4,3,2,1,0:T(8,128)S(1)}, f32[1,4,2,160,96]{4,3,2,1,0:T(8,128)}, u32[]{:S(2)}) copy-start(f32[1,4,2,160,96]{4,3,2,1,0:T(8,128)} %param.13) | copy-start | bytes 1474564
  3.6 18.9 %collective-permute-start = (f32[1,2,2,160,96]{4,3,2,1,0:T(8,128)S(1)}, f32[1,2,2,160,96]{4,3,2,1,0:T(8,128)S(1)}, u32[]{:S(2)}, u32[]{:S(2)}) collective-permute-start(f32[1,2,2,160,96]{4,3,2,1,0:T(8,128)S(1)} %slice.192), channel_id=1, source_target_pairs={{0,4},{4,8},{8,12},{12,16},{16,20},{20,24},{24,28},{1,5},{5,9},{9,... | collective-permute-start | bytes 737288 | tf_op jit(solution)/shard_map/ppermute | solution.py:12
  8.5 13.9 %collective-permute-start.1 = (f32[1,2,2,160,96]{4,3,2,1,0:T(8,128)S(1)}, f32[1,2,2,160,96]{4,3,2,1,0:T(8,128)S(1)}, u32[]{:S(2)}, u32[]{:S(2)}) collective-permute-start(f32[1,2,2,160,96]{4,3,2,1,0:T(8,128)S(1)} %slice.145), channel_id=1, source_target_pairs={{4,0},{8,4},{12,8},{16,12},{20,16},{24,20},{28,24},{5,1},{9,5},{13... | collective-permute-start | bytes 737288 | tf_op jit(solution)/shard_map/ppermute | solution.py:12
  22.4 0.7 copy-start.8
  23.3 1.7 copy-start.7
  24.4 11.4 %collective-permute-start.2 = (f32[2,6,1,160,96]{4,3,2,1,0:T(8,128)}, f32[2,6,1,160,96]{4,3,2,1,0:T(8,128)}, u32[]{:S(2)}, u32[]{:S(2)}) collective-permute-start(f32[2,6,1,160,96]{4,3,2,1,0:T(8,128)} %slice_select_fusion), channel_id=1, source_target_pairs={{0,2},{2,0},{1,3},{3,1},{4,6},{6,4},{5,7},{7,5},{8,10},{10,8},{9,1... | collective-permute-start | bytes 2211848 | tf_op jit(solution)/shard_map/ppermute | solution.py:22
  35.8 1.5 copy-start.9
  42.5 7.1 %copy-start.5 = (f32[864,288,1,1]{0,1,2,3:T(8,128)S(1)}, f32[864,288,1,1]{0,1,2,3:T(8,128)}, u32[]{:S(2)}) copy-start(f32[864,288,1,1]{0,1,2,3:T(8,128)} %reshape.169) | copy-start | bytes 2985988
  49.5 6.2 %copy-start.12 = (f32[96]{0:T(128)S(1)}, f32[96]{0:T(128)}, u32[]{:S(2)}) copy-start(f32[96]{0:T(128)} %param.9) | copy-start | bytes 1156
  56.5 7.1 %copy-start.4 = (f32[864,288,1,1]{0,1,2,3:T(8,128)S(1)}, f32[864,288,1,1]{0,1,2,3:T(8,128)}, u32[]{:S(2)}) copy-start(f32[864,288,1,1]{0,1,2,3:T(8,128)} %reshape.168) | copy-start | bytes 2985988
  63.6 6.6 %copy-start.11 = (f32[96]{0:T(128)S(1)}, f32[96]{0:T(128)}, u32[]{:S(2)}) copy-start(f32[96]{0:T(128)} %param.12) | copy-start | bytes 1156
  63.6 11.7 %slice-start = ((s8[4816896]{0:T(1024)(128)(4,1)}), s8[4194304]{0:T(1024)(128)(4,1)S(1)}, s32[]{:S(2)}) async-start(s8[4816896]{0:T(1024)(128)(4,1)} %bitcast.83), calls=%async_computation | async-start | bytes 8388608
  70.2 5.1 %slice-start.1 = ((s8[4816896]{0:T(1024)(128)(4,1)}), s8[622592]{0:T(1024)(128)(4,1)S(1)}, s32[]{:S(2)}) async-start(s8[4816896]{0:T(1024)(128)(4,1)} %bitcast.83), calls=%async_computation.1 | async-start | bytes 1245184
  74.0 14.1 %collective-permute-start.3 = (f32[1,2,2,160,96]{4,3,2,1,0:T(8,128)}, f32[1,2,2,160,96]{4,3,2,1,0:T(8,128)}, u32[]{:S(2)}, u32[]{:S(2)}) collective-permute-start(f32[1,2,2,160,96]{4,3,2,1,0:T(8,128)} %slice.203), channel_id=1, source_target_pairs={{4,0},{8,4},{12,8},{16,12},{20,16},{24,20},{28,24},{5,1},{9,5},{13... | collective-permute-start | bytes 737288 | tf_op jit(solution)/shard_map/ppermute | solution.py:12
  84.4 3.0 %copy-start.6 = (f32[1,4,2,160,96]{4,3,2,1,0:T(8,128)S(1)}, f32[1,4,2,160,96]{4,3,2,1,0:T(8,128)}, u32[]{:S(2)}) copy-start(f32[1,4,2,160,96]{4,3,2,1,0:T(8,128)} %get-tuple-element.63) | copy-start | bytes 1474564
  90.0 13.1 %collective-permute-start.4 = (f32[1,6,1,160,96]{4,3,2,1,0:T(8,128)}, f32[1,6,1,160,96]{4,3,2,1,0:T(8,128)}, u32[]{:S(2)}, u32[]{:S(2)}) collective-permute-start(f32[1,6,1,160,96]{4,3,2,1,0:T(8,128)} %fusion.29), channel_id=1, source_target_pairs={{0,2},{2,0},{1,3},{3,1},{4,6},{6,4},{5,7},{7,5},{8,10},{10,8},{9,1... | collective-permute-start | bytes 1105928 | tf_op jit(solution)/shard_map/ppermute | solution.py:22
  107.9 7.0 %copy-start.3 = (f32[864,288,1,1]{0,1,2,3:T(8,128)S(1)}, f32[864,288,1,1]{0,1,2,3:T(8,128)}, u32[]{:S(2)}) copy-start(f32[864,288,1,1]{0,1,2,3:T(8,128)} %reshape.170) | copy-start | bytes 2985988
  114.9 6.3 %copy-start = (f32[1,4,2,160,96]{4,3,2,1,0:T(8,128)S(1)}, f32[1,4,2,160,96]{4,3,2,1,0:T(8,128)}, u32[]{:S(2)}) copy-start(f32[1,4,2,160,96]{4,3,2,1,0:T(8,128)} %param.7) | copy-start | bytes 1474564
  114.9 6.3 %copy-start.10 = (f32[96]{0:T(128)S(1)}, f32[96]{0:T(128)}, u32[]{:S(2)}) copy-start(f32[96]{0:T(128)} %param.10) | copy-start | bytes 1156
  122.3 1.4 copy-start.2
  132.7 3.0 %collective-permute-start.5 = (f32[1,8,326,96]{2,3,1,0:T(8,128)S(1)}, f32[1,8,326,96]{2,3,1,0:T(8,128)S(1)}, u32[]{:S(2)}, u32[]{:S(2)}) collective-permute-start(f32[1,8,326,96]{2,3,1,0:T(8,128)S(1)} %bitcast.95), channel_id=1, source_target_pairs={{0,2},{2,0},{1,3},{3,1},{4,6},{6,4},{5,7},{7,5},{8,10},{10,8},{9,1... | collective-permute-start | bytes 3004424 | tf_op jit(solution)/shard_map/ppermute | solution.py:90
  135.9 17.0 %collective-permute-start.6 = (f32[4,326,96]{1,2,0:T(8,128)S(1)}, f32[4,326,96]{1,2,0:T(8,128)S(1)}, u32[]{:S(2)}, u32[]{:S(2)}) collective-permute-start(f32[4,326,96]{1,2,0:T(8,128)S(1)} %dynamic-slice_bitcast_fusion), channel_id=1, source_target_pairs={{0,4},{4,0},{8,12},{12,8},{16,20},{20,16},{24,28},{28,24},{1,5},{5... | collective-permute-start | bytes 1502216 | tf_op jit(solution)/shard_map/ppermute | solution.py:90
  153.0 9.9 %collective-permute-start.7 = (f32[2,326,96]{1,2,0:T(8,128)S(1)}, f32[2,326,96]{1,2,0:T(8,128)S(1)}, u32[]{:S(2)}, u32[]{:S(2)}) collective-permute-start(f32[2,326,96]{1,2,0:T(8,128)S(1)} %dynamic-slice_bitcast_fusion.1), channel_id=1, source_target_pairs={{0,8},{4,12},{8,0},{12,4},{16,24},{20,28},{24,16},{28,20},{1,9},{5... | collective-permute-start | bytes 751112 | tf_op jit(solution)/shard_map/ppermute | solution.py:90
  163.1 9.9 %collective-permute-start.8 = (f32[1,326,96]{1,2,0:T(8,128)S(1)}, f32[1,326,96]{1,2,0:T(8,128)S(1)}, u32[]{:S(2)}, u32[]{:S(2)}) collective-permute-start(f32[1,326,96]{1,2,0:T(8,128)S(1)} %constant_dynamic-slice_fusion), channel_id=1, source_target_pairs={{0,16},{4,20},{8,24},{12,28},{16,0},{20,4},{24,8},{28,12},{1,17},{... | collective-permute-start | bytes 375560 | tf_op jit(solution)/shard_map/ppermute | solution.py:90
  172.9 5.2 %collective-permute-start.9 = (f32[326,96]{0,1:T(8,128)S(1)}, f32[326,96]{0,1:T(8,128)S(1)}, u32[]{:S(2)}, u32[]{:S(2)}) collective-permute-start(f32[326,96]{0,1:T(8,128)S(1)} %add_bitcast_fusion), channel_id=1, source_target_pairs={{0,1},{1,0},{2,3},{3,2},{4,5},{5,4},{6,7},{7,6},{8,9},{9,8},{10,11... | collective-permute-start | bytes 375560 | tf_op jit(solution)/shard_map/ppermute | solution.py:90
  178.2 1.4 collective-permute-start.10

commit v3 on v2

--- a/solution.py
+++ b/solution.py
@@ -106,6 +106,36 @@
     return blocks[0]
 
 
+def swapped_low(t):
+    return t - t % 4 + (t % 2) * 2 + (t // 2) % 2
+
+
+def halved_across(blocks):
+    count = lax.axis_size("tm")
+    heights = lax.axis_size("height")
+    if count & (count - 1) or count < 4 or heights < 2:
+        return halved(blocks, "tm")
+    odd = lax.axis_index("height") % 2 == 1
+    order = [swapped_low(k) for k in range(count)]
+    blocks = jnp.where(odd, jnp.stack([blocks[k] for k in order]), blocks)
+    me = lax.axis_index("tm")
+    label = jnp.where(odd, swapped_low(me), me)
+    bit = 1
+    while bit < count:
+        mine = (label // bit) % 2
+        pairs = blocks.reshape((blocks.shape[0] // 2, 2) + blocks.shape[1:])
+        keep = lax.dynamic_index_in_dim(pairs, mine, axis=1, keepdims=False)
+        send = lax.dynamic_index_in_dim(pairs, 1 - mine, axis=1, keepdims=False)
+        route = []
+        for t in range(count):
+            for h in range(heights):
+                relabel = swapped_low if h % 2 else (lambda v: v)
+                route.append((t * heights + h, relabel(relabel(t) ^ bit) * heights + h))
+        blocks = keep + lax.ppermute(send, ("tm", "height"), route)
+        bit *= 2
+    return blocks[0]
+
+
 def summed(block, axis):
     count = lax.axis_size(axis)
     if count & (count - 1):
@@ -137,7 +167,7 @@
     width = -(-size // split)
     blocks = jnp.pad(blocks, ((0, 0), (0, width * split - size), (0, 0)))
     blocks = jnp.swapaxes(blocks.reshape(parts, split, width, channels), 0, 1)
-    block = halved(halved(blocks, "height"), "tm")
+    block = halved_across(halved(blocks, "height"))
     return gathered(summed(block, "batch"), "height")[:size]
 
 

time: 183 us -> 175 us (0.956)
  waiting for transfers between devices: 47 us -> 38.8 us
    ppermute x6 -> x3, waiting for transfers between devices: 34.4 us -> 7.45 us  [exchanged(): return lax.ppermute(block, axis, [(i, i ^ bit) for i in range(count)])]
    ppermute x0 -> x3, waiting for transfers between devices: none -> 18.8 us  [halved_across(): blocks = keep + lax.ppermute(send, ('tm', 'height'), route)]
    ppermute x6 -> x3, starting transfers between devices: 12.1 us -> 2.22 us  [exchanged(): return lax.ppermute(block, axis, [(i, i ^ bit) for i in range(count)])]
    ppermute x0 -> x3, starting transfers between devices: none -> 9.81 us  [halved_across(): blocks = keep + lax.ppermute(send, ('tm', 'height'), route)]
  transfers between devices with their start and end apart: 11 -> 11, of which waited for: 7 -> 7; matrix products, arithmetic and copies ran while one was open for 20% -> 21% of each run, Pallas kernels for 0% -> 0%
where the time goes in v3:
time: 175 us; the launch traced here: 173 us
  local copies, waits for them, and re-layouts  63.2 us (36%)
  waiting for transfers between devices  38.8 us (22%)
  matrix products  29.7 us (17%)
  other arithmetic  20.8 us (12%)
  starting transfers between devices  19.5 us (11%)
    concatenate x3, local copies, waits for them, and re-layouts, row_patches(): taps = jnp.concatenate(pieces, axis=-1)  21.1 us
    dot_general x3, matrix products, conv_rows(): out = jnp.dot(taps, stacked, precision=lax.Precision.HIGH)  19 us
    ppermute x3, waiting for transfers between devices, halved_across(): blocks = keep + lax.ppermute(send, ('tm', 'height'), route)  18.8 us
    ppermute x3, waiting for transfers between devices, passed_along(): return lax.ppermute(block, axis, route)  12.6 us
    dot_general x2, matrix products, kernel_grad_rows(): jnp.dot(flat, taps, precision=lax.Precision.HIGH)  10.7 us
    ppermute x3, starting transfers between devices, halved_across(): blocks = keep + lax.ppermute(send, ('tm', 'height'), route)  9.81 us
    ppermute x3, starting transfers between devices, passed_along(): return lax.ppermute(block, axis, route)  7.46 us
    ppermute x3, waiting for transfers between devices, exchanged(): return lax.ppermute(block, axis, [(i, i ^ bit) for i in range(count)])  7.45 us
  transfers between devices with their start and end apart: 11, of which 7 were waited for; matrix products, arithmetic and copies ran while one was open for 21% of the time, Pallas kernels for 0%

profile of v3, /device:TPU:0, one launch (start us, length us, event | category | flops | bytes accessed | tf_op | source)
XLA Modules:
  0.0 173.3 jit_solution(2670145157341644415)
XLA Ops:
  3.6 4.9 %collective-permute-start = (f32[1,2,2,160,96]{4,3,2,1,0:T(8,128)S(1)}, f32[1,2,2,160,96]{4,3,2,1,0:T(8,128)S(1)}, u32[]{:S(2)}, u32[]{:S(2)}) collective-permute-start(f32[1,2,2,160,96]{4,3,2,1,0:T(8,128)S(1)} %slice.256), channel_id=1, source_target_pairs={{0,4},{4,8},{8,12},{12,16},{16,20},{20,24},{24,28},{1,5},{5,9},{9,... | collective-permute-start | bytes 737288 | tf_op jit(solution)/shard_map/ppermute | solution.py:12
  9.8 12.6 %collective-permute-done = f32[1,2,2,160,96]{4,3,2,1,0:T(8,128)S(1)} collective-permute-done((f32[1,2,2,160,96]{4,3,2,1,0:T(8,128)S(1)}, f32[1,2,2,160,96]{4,3,2,1,0:T(8,128)S(1)}, u32[]{:S(2)}, u32[]{:S(2)}) %collective-permute-start) | collective-permute-done | bytes 245792 | tf_op jit(solution)/shard_map/ppermute | solution.py:12
  26.0 1.6 reshape.179
  27.6 2.6 %copy.29 = f32[3,3,96,3,96]{2,1,0,4,3:T(4,128)S(1)} copy(f32[3,3,96,3,96]{4,2,3,1,0:T(8,128)} %bitcast.124) | data formatting | bytes 1990656 | tf_op jit(solution)/shard_map/transpose | solution.py:53
  30.2 1.6 reshape.180
  34.2 1.6 reshape.181
  37.9 4.5 %pad_slice_fusion = (f32[1,4,2,168,96]{4,3,2,1,0:T(8,128)}, f32[1,4,2,168,96]{4,3,2,1,0:T(8,128)}, f32[1,4,2,168,96]{4,3,2,1,0:T(8,128)}, f32[1,4,2,168,96]{4,3,...) fusion(f32[1,6,4,160,96]{4,3,2,1,0:T(8,128)S(1)} %get-tuple-ele, ...), kind=kLoop, calls=%fused_computation.27 | loop fusion | bytes 12238848 | tf_op jit(solution)/shard_map/slice | solution.py:45
  42.5 7.1 %concatenate.47 = f32[1,4,2,168,864]{4,3,2,1,0:T(8,128)} concatenate(f32[1,4,2,168,96]{4,3,2,1,0:T(8,128)} %get-tuple-element.60, f32[1,4,2,168,96]{4,3,2,1,0:T(8,128)} %get-tuple-element.53, f32[1,4,2,168,96]{4,3,2,1,0:T(8,128)} %get-tuple-element.54, f32[1,4,2,168,96]{4,3,2,1,0:T(8,128)} %get-tuple-element.55, f32[1,4,2,168,96]{4,3,2,1,0:T(8,128)} %get-tuple-element.56, ...), dimensions={4} | concatenate | bytes 9289728 | tf_op jit(solution)/shard_map/concatenate | solution.py:46
  49.5 6.2 %fusion.11 = f32[1,4,2,168,288]{4,3,2,1,0:T(8,128)S(1)} fusion(f32[1,4,2,168,864]{4,3,2,1,0:T(8,128)} %concatenate.47, f32[864,288,1,1]{0,1,2,3:T(8,128)S(1)} %copy-done.5), kind=kOutput, calls=%fused_computation.25 | convolution fusion | flops 2006581248 | bytes 7188480 | tf_op jit(solution)/shard_map/dot_general | solution.py:54
  56.5 7.1 %concatenate.46 = f32[1,4,2,168,864]{4,3,2,1,0:T(8,128)} concatenate(f32[1,4,2,168,96]{4,3,2,1,0:T(8,128)} %get-tuple-element.70, f32[1,4,2,168,96]{4,3,2,1,0:T(8,128)} %get-tuple-element.77, f32[1,4,2,168,96]{4,3,2,1,0:T(8,128)} %get-tuple-element.76, f32[1,4,2,168,96]{4,3,2,1,0:T(8,128)} %get-tuple-element.75, f32[1,4,2,168,96]{4,3,2,1,0:T(8,128)} %get-tuple-element.74, ...), dimensions={4} | concatenate | bytes 9289728 | tf_op jit(solution)/shard_map/concatenate | solution.py:46
  63.6 6.5 %fusion.8 = f32[1,4,2,168,288]{4,3,2,1,0:T(8,128)S(1)} fusion(f32[1,4,2,168,864]{4,3,2,1,0:T(8,128)} %concatenate.46, f32[864,288,1,1]{0,1,2,3:T(8,128)S(1)} %copy-done.4), kind=kOutput, calls=%fused_computation.24 | convolution fusion | flops 2006581248 | bytes 7188480 | tf_op jit(solution)/shard_map/dot_general | solution.py:54
  70.2 1.7 %multiply_reduce_fusion = (f32[96]{0:T(128)S(1)}, f32[4,2,160]{2,1,0:T(2,128)S(1)}, f32[1,4,2,160,96]{4,3,2,1,0:T(8,128)S(1)}, f32[1,4,2,160,96]{4,3,2,1,0:T(8,128)}) fusion(f32[1,4,2,160,96]{4,3,2,1,0:T(8,128)S(1)} %get-tuple-element.29, f32[4,2,160]{2,1,0:T(2,128)S(1)} %fusion.39, f32[96]{0:T(128)S(1)} %copy-done.11, f32[1,4,2,168,288]{4,3,2,1,0:T(8,128)S(1)} %fusion.8), kind=kLoop, calls=%fused_computation.71 | loop fusion | flops 2333344 | bytes 2960128 | tf_op jit(solution)/shard_map/transpose(jvp())/reduce_sum | solution.py:37
  75.4 4.3 %fusion.48 = f32[288,864]{1,0:T(8,128)} fusion(f32[288,1344]{0,1:T(8,128)S(1)} %bitcast.121, f32[1344,864]{1,0:T(8,128)S(1)} %bitcast.118), kind=kOutput, calls=%fused_computation.126 | convolution fusion | flops 2006581248 | bytes 7188480 | tf_op jit(solution)/shard_map/dot_general | solution.py:69
  79.6 2.5 %reshape.174 = f32[3,96,3,3,96]{4,3,2,1,0:T(4,128)S(1)} reshape(f32[288,864]{1,0:T(8,128)} %fusion.48) | data formatting | bytes 1990656 | tf_op jit(solution)/shard_map/reshape | solution.py:70
  82.2 2.2 %copy.31 = f32[3,3,3,96,96]{4,3,2,1,0:T(8,128)} copy(f32[3,3,3,96,96]{3,1,0,4,2:T(4,128)S(1)} %bitcast.122) | data formatting | bytes 1990656 | tf_op jit(solution)/shard_map/transpose | solution.py:76
  88.2 1.8 %fusion.29 = f32[1,6,1,160,96]{4,3,2,1,0:T(8,128)} fusion(f32[1,4,2,160,96]{4,3,2,1,0:T(8,128)S(1)} %get-tuple-element.25, f32[1,2,2,160,96]{4,3,2,1,0:T(8,128)} %collective-permute-done.3, pred[]{:T(512)S(6)} %eq.20), kind=kLoop, calls=%fused_computation.85 | loop fusion | flops 276480 | bytes 1105921 | tf_op jit(solution)/shard_map/jit(_where)/select_n | solution.py:22
  90.0 6.4 %fusion.49 = f32[288,864]{1,0:T(8,128)} fusion(f32[288,1344]{0,1:T(8,128)S(1)} %bitcast.120, f32[1344,864]{1,0:T(8,128)} %bitcast.115), kind=kOutput, calls=%fused_computation.127 | convolution fusion | flops 2006581248 | bytes 7188480 | tf_op jit(solution)/shard_map/dot_general | solution.py:69
  96.4 2.5 %reshape.177 = f32[3,96,3,3,96]{4,3,2,1,0:T(4,128)S(1)} reshape(f32[288,864]{1,0:T(8,128)} %fusion.49) | data formatting | bytes 1990656 | tf_op jit(solution)/shard_map/reshape | solution.py:70
  105.4 2.5 %fusion.45 = (f32[1,4,2,168,96]{4,3,2,1,0:T(8,128)S(1)}, f32[1,4,2,168,96]{4,3,2,1,0:T(8,128)}, f32[1,4,2,168,96]{4,3,2,1,0:T(8,128)}, f32[1,4,2,168,96]{4,3,2,1...) fusion(f32[1,6,4,168,96]{4,3,2,1,0:T(8,128)S(1)} %select_maximu, ...), kind=kLoop, calls=%fused_computation.123 | loop fusion | bytes 9289728 | tf_op jit(solution)/shard_map/slice | solution.py:45
  107.9 7.0 %concatenate.50 = f32[1,4,2,168,864]{4,3,2,1,0:T(8,128)} concatenate(f32[1,4,2,168,96]{4,3,2,1,0:T(8,128)} %get-tuple-element.42, f32[1,4,2,168,96]{4,3,2,1,0:T(8,128)} %get-tuple-element.41, f32[1,4,2,168,96]{4,3,2,1,0:T(8,128)} %get-tuple-element.40, f32[1,4,2,168,96]{4,3,2,1,0:T(8,128)} %get-tuple-element.39, f32[1,4,2,168,96]{4,3,2,1,0:T(8,128)} %get-tuple-element.38, ...), dimensions={4} | concatenate | bytes 9289728 | tf_op jit(solution)/shard_map/concatenate | solution.py:46
  115.0 6.3 %fusion.14 = f32[1,4,2,168,288]{4,3,2,1,0:T(8,128)S(1)} fusion(f32[1,4,2,168,864]{4,3,2,1,0:T(8,128)} %concatenate.50, f32[864,288,1,1]{0,1,2,3:T(8,128)S(1)} %copy-done.3), kind=kOutput, calls=%fused_computation.26 | convolution fusion | flops 2006581248 | bytes 7188480 | tf_op jit(solution)/shard_map/dot_general | solution.py:54
  123.7 3.3 %maximum_multiply_fusion = f32[8,652,96]{1,2,0:T(8,128)} fusion(f32[8,4,96]{1,2,0:T(8,128)S(1)} %broadcast_in_dim.14, f32[8,324,96]{1,2,0:T(8,128)} %copy.35, f32[8,324,96]{1,2,0:T(8,128)S(1)} %copy-done.2), kind=kLoop, calls=%fused_computation.11 | loop fusion | flops 1502208 | bytes 4005888 | tf_op jit(solution)/shard_map/mul | solution.py:231
  127.0 3.3 %mul.212 = f32[8,2,326,96]{2,1,3,0:T(2,128)S(1)} reshape(f32[8,652,96]{1,2,0:T(8,128)} %maximum_multiply_fusion) | data formatting | bytes 4005888 | tf_op jit(solution)/shard_map/mul | solution.py:231
  130.3 2.3 %constant_dynamic-slice_fusion.2 = (f32[8,1,326,96]{2,1,3,0:T(1,128)S(1)}, f32[8,1,326,96]{2,1,3,0:T(1,128)S(1)}) fusion(f32[8,2,326,96]{2,1,3,0:T(2,128)S(1)} %mul.212, s32[]{:T(128)S(6)} %select_n.139, s32[]{:T(128)S(6)} %select_n.140), kind=kLoop, calls=%fused_computation.120 | loop fusion | bytes 4005896 | tf_op jit(solution)/shard_map/dynamic-slice.4
  133.2 2.5 %collective-permute-done.5 = f32[1,8,326,96]{2,3,1,0:T(8,128)S(1)} collective-permute-done((f32[1,8,326,96]{2,3,1,0:T(8,128)S(1)}, f32[1,8,326,96]{2,3,1,0:T(8,128)S(1)}, u32[]{:S(2)}, u32[]{:S(2)}) %collective-permute-start.5) | collective-permute-done | bytes 1001504 | tf_op jit(solution)/shard_map/ppermute | solution.py:90
  136.2 3.2 %collective-permute-start.6 = (f32[4,326,96]{1,2,0:T(8,128)S(1)}, f32[4,326,96]{1,2,0:T(8,128)S(1)}, u32[]{:S(2)}, u32[]{:S(2)}) collective-permute-start(f32[4,326,96]{1,2,0:T(8,128)S(1)} %dynamic-slice_bitcast_fusion), channel_id=1, source_target_pairs={{0,4},{2,10},{4,0},{6,14},{8,12},{10,2},{12,8},{14,6},{16,20},{18,... | collective-permute-start | bytes 1502216 | tf_op jit(solution)/shard_map/ppermute | solution.py:134
  139.4 7.9 %collective-permute-done.6 = f32[4,326,96]{1,2,0:T(8,128)S(1)} collective-permute-done((f32[4,326,96]{1,2,0:T(8,128)S(1)}, f32[4,326,96]{1,2,0:T(8,128)S(1)}, u32[]{:S(2)}, u32[]{:S(2)}) %collective-permute-start.6) | collective-permute-done | bytes 500768 | tf_op jit(solution)/shard_map/ppermute | solution.py:134
  147.3 3.5 %collective-permute-start.7 = (f32[2,326,96]{1,2,0:T(8,128)S(1)}, f32[2,326,96]{1,2,0:T(8,128)S(1)}, u32[]{:S(2)}, u32[]{:S(2)}) collective-permute-start(f32[2,326,96]{1,2,0:T(8,128)S(1)} %dynamic-slice_bitcast_fusion.1), channel_id=1, source_target_pairs={{0,8},{2,6},{4,12},{6,2},{8,0},{10,14},{12,4},{14,10},{16,24},{18,... | collective-permute-start | bytes 751112 | tf_op jit(solution)/shard_map/ppermute | solution.py:134
  150.9 4.7 %collective-permute-done.7 = f32[2,326,96]{1,2,0:T(8,128)S(1)} collective-permute-done((f32[2,326,96]{1,2,0:T(8,128)S(1)}, f32[2,326,96]{1,2,0:T(8,128)S(1)}, u32[]{:S(2)}, u32[]{:S(2)}) %collective-permute-start.7) | collective-permute-done | bytes 250400 | tf_op jit(solution)/shard_map/ppermute | solution.py:134
  155.6 3.1 %collective-permute-start.8 = (f32[1,326,96]{1,2,0:T(8,128)S(1)}, f32[1,326,96]{1,2,0:T(8,128)S(1)}, u32[]{:S(2)}, u32[]{:S(2)}) collective-permute-start(f32[1,326,96]{1,2,0:T(8,128)S(1)} %constant_dynamic-slice_fusion), channel_id=1, source_target_pairs={{0,16},{2,18},{4,20},{6,22},{8,24},{10,26},{12,28},{14,30},{16,0},... | collective-permute-start | bytes 375560 | tf_op jit(solution)/shard_map/ppermute | solution.py:134
  158.7 6.2 %collective-permute-done.8 = f32[1,326,96]{1,2,0:T(8,128)S(1)} collective-permute-done((f32[1,326,96]{1,2,0:T(8,128)S(1)}, f32[1,326,96]{1,2,0:T(8,128)S(1)}, u32[]{:S(2)}, u32[]{:S(2)}) %collective-permute-start.8) | collective-permute-done | bytes 125216 | tf_op jit(solution)/shard_map/ppermute | solution.py:134
  166.5 3.6 %collective-permute-done.9 = f32[326,96]{0,1:T(8,128)S(1)} collective-permute-done((f32[326,96]{0,1:T(8,128)S(1)}, f32[326,96]{0,1:T(8,128)S(1)}, u32[]{:S(2)}, u32[]{:S(2)}) %collective-permute-start.9) | collective-permute-done | bytes 125216 | tf_op jit(solution)/shard_map/ppermute | solution.py:90
  (99 shorter events, 34.9 us)
Async XLA Ops:
  0.6 7.8 %copy-start.1 = (f32[1,4,2,160,96]{4,3,2,1,0:T(8,128)S(1)}, f32[1,4,2,160,96]{4,3,2,1,0:T(8,128)}, u32[]{:S(2)}) copy-start(f32[1,4,2,160,96]{4,3,2,1,0:T(8,128)} %param.13) | copy-start | bytes 1474564
  3.6 18.9 %collective-permute-start = (f32[1,2,2,160,96]{4,3,2,1,0:T(8,128)S(1)}, f32[1,2,2,160,96]{4,3,2,1,0:T(8,128)S(1)}, u32[]{:S(2)}, u32[]{:S(2)}) collective-permute-start(f32[1,2,2,160,96]{4,3,2,1,0:T(8,128)S(1)} %slice.256), channel_id=1, source_target_pairs={{0,4},{4,8},{8,12},{12,16},{16,20},{20,24},{24,28},{1,5},{5,9},{9,... | collective-permute-start | bytes 737288 | tf_op jit(solution)/shard_map/ppermute | solution.py:12
  8.5 13.9 %collective-permute-start.1 = (f32[1,2,2,160,96]{4,3,2,1,0:T(8,128)S(1)}, f32[1,2,2,160,96]{4,3,2,1,0:T(8,128)S(1)}, u32[]{:S(2)}, u32[]{:S(2)}) collective-permute-start(f32[1,2,2,160,96]{4,3,2,1,0:T(8,128)S(1)} %slice.193), channel_id=1, source_target_pairs={{4,0},{8,4},{12,8},{16,12},{20,16},{24,20},{28,24},{5,1},{9,5},{13... | collective-permute-start | bytes 737288 | tf_op jit(solution)/shard_map/ppermute | solution.py:12
  22.4 0.7 copy-start.8
  23.3 1.7 copy-start.7
  24.4 11.4 %collective-permute-start.2 = (f32[2,6,1,160,96]{4,3,2,1,0:T(8,128)}, f32[2,6,1,160,96]{4,3,2,1,0:T(8,128)}, u32[]{:S(2)}, u32[]{:S(2)}) collective-permute-start(f32[2,6,1,160,96]{4,3,2,1,0:T(8,128)} %slice_select_fusion), channel_id=1, source_target_pairs={{0,2},{2,0},{1,3},{3,1},{4,6},{6,4},{5,7},{7,5},{8,10},{10,8},{9,1... | collective-permute-start | bytes 2211848 | tf_op jit(solution)/shard_map/ppermute | solution.py:22
  35.8 1.5 copy-start.9
  42.5 7.1 %copy-start.5 = (f32[864,288,1,1]{0,1,2,3:T(8,128)S(1)}, f32[864,288,1,1]{0,1,2,3:T(8,128)}, u32[]{:S(2)}) copy-start(f32[864,288,1,1]{0,1,2,3:T(8,128)} %reshape.180) | copy-start | bytes 2985988
  49.5 6.2 %copy-start.12 = (f32[96]{0:T(128)S(1)}, f32[96]{0:T(128)}, u32[]{:S(2)}) copy-start(f32[96]{0:T(128)} %param.9) | copy-start | bytes 1156
  56.5 7.1 %copy-start.4 = (f32[864,288,1,1]{0,1,2,3:T(8,128)S(1)}, f32[864,288,1,1]{0,1,2,3:T(8,128)}, u32[]{:S(2)}) copy-start(f32[864,288,1,1]{0,1,2,3:T(8,128)} %reshape.179) | copy-start | bytes 2985988
  63.6 6.6 %copy-start.11 = (f32[96]{0:T(128)S(1)}, f32[96]{0:T(128)}, u32[]{:S(2)}) copy-start(f32[96]{0:T(128)} %param.12) | copy-start | bytes 1156
  63.6 11.7 %slice-start = ((s8[4816896]{0:T(1024)(128)(4,1)}), s8[4194304]{0:T(1024)(128)(4,1)S(1)}, s32[]{:S(2)}) async-start(s8[4816896]{0:T(1024)(128)(4,1)} %bitcast.116), calls=%async_computation | async-start | bytes 8388608
  70.2 5.1 %slice-start.1 = ((s8[4816896]{0:T(1024)(128)(4,1)}), s8[622592]{0:T(1024)(128)(4,1)S(1)}, s32[]{:S(2)}) async-start(s8[4816896]{0:T(1024)(128)(4,1)} %bitcast.116), calls=%async_computation.1 | async-start | bytes 1245184
  74.0 14.1 %collective-permute-start.3 = (f32[1,2,2,160,96]{4,3,2,1,0:T(8,128)}, f32[1,2,2,160,96]{4,3,2,1,0:T(8,128)}, u32[]{:S(2)}, u32[]{:S(2)}) collective-permute-start(f32[1,2,2,160,96]{4,3,2,1,0:T(8,128)} %slice.267), channel_id=1, source_target_pairs={{4,0},{8,4},{12,8},{16,12},{20,16},{24,20},{28,24},{5,1},{9,5},{13... | collective-permute-start | bytes 737288 | tf_op jit(solution)/shard_map/ppermute | solution.py:12
  84.4 3.0 %copy-start.6 = (f32[1,4,2,160,96]{4,3,2,1,0:T(8,128)S(1)}, f32[1,4,2,160,96]{4,3,2,1,0:T(8,128)}, u32[]{:S(2)}) copy-start(f32[1,4,2,160,96]{4,3,2,1,0:T(8,128)} %get-tuple-element.63) | copy-start | bytes 1474564
  90.0 13.1 %collective-permute-start.4 = (f32[1,6,1,160,96]{4,3,2,1,0:T(8,128)}, f32[1,6,1,160,96]{4,3,2,1,0:T(8,128)}, u32[]{:S(2)}, u32[]{:S(2)}) collective-permute-start(f32[1,6,1,160,96]{4,3,2,1,0:T(8,128)} %fusion.29), channel_id=1, source_target_pairs={{0,2},{2,0},{1,3},{3,1},{4,6},{6,4},{5,7},{7,5},{8,10},{10,8},{9,1... | collective-permute-start | bytes 1105928 | tf_op jit(solution)/shard_map/ppermute | solution.py:22
  107.9 7.0 %copy-start.3 = (f32[864,288,1,1]{0,1,2,3:T(8,128)S(1)}, f32[864,288,1,1]{0,1,2,3:T(8,128)}, u32[]{:S(2)}) copy-start(f32[864,288,1,1]{0,1,2,3:T(8,128)} %reshape.181) | copy-start | bytes 2985988
  114.9 6.3 %copy-start = (f32[1,4,2,160,96]{4,3,2,1,0:T(8,128)S(1)}, f32[1,4,2,160,96]{4,3,2,1,0:T(8,128)}, u32[]{:S(2)}) copy-start(f32[1,4,2,160,96]{4,3,2,1,0:T(8,128)} %param.7) | copy-start | bytes 1474564
  114.9 6.3 %copy-start.10 = (f32[96]{0:T(128)S(1)}, f32[96]{0:T(128)}, u32[]{:S(2)}) copy-start(f32[96]{0:T(128)} %param.10) | copy-start | bytes 1156
  122.3 1.4 copy-start.2
  132.7 3.0 %collective-permute-start.5 = (f32[1,8,326,96]{2,3,1,0:T(8,128)S(1)}, f32[1,8,326,96]{2,3,1,0:T(8,128)S(1)}, u32[]{:S(2)}, u32[]{:S(2)}) collective-permute-start(f32[1,8,326,96]{2,3,1,0:T(8,128)S(1)} %bitcast.128), channel_id=1, source_target_pairs={{0,2},{2,0},{1,3},{3,1},{4,6},{6,4},{5,7},{7,5},{8,10},{10,8},{9,1... | collective-permute-start | bytes 3004424 | tf_op jit(solution)/shard_map/ppermute | solution.py:90
  136.2 11.0 %collective-permute-start.6 = (f32[4,326,96]{1,2,0:T(8,128)S(1)}, f32[4,326,96]{1,2,0:T(8,128)S(1)}, u32[]{:S(2)}, u32[]{:S(2)}) collective-permute-start(f32[4,326,96]{1,2,0:T(8,128)S(1)} %dynamic-slice_bitcast_fusion), channel_id=1, source_target_pairs={{0,4},{2,10},{4,0},{6,14},{8,12},{10,2},{12,8},{14,6},{16,20},{18,... | collective-permute-start | bytes 1502216 | tf_op jit(solution)/shard_map/ppermute | solution.py:134
  147.3 8.2 %collective-permute-start.7 = (f32[2,326,96]{1,2,0:T(8,128)S(1)}, f32[2,326,96]{1,2,0:T(8,128)S(1)}, u32[]{:S(2)}, u32[]{:S(2)}) collective-permute-start(f32[2,326,96]{1,2,0:T(8,128)S(1)} %dynamic-slice_bitcast_fusion.1), channel_id=1, source_target_pairs={{0,8},{2,6},{4,12},{6,2},{8,0},{10,14},{12,4},{14,10},{16,24},{18,... | collective-permute-start | bytes 751112 | tf_op jit(solution)/shard_map/ppermute | solution.py:134
  155.6 9.3 %collective-permute-start.8 = (f32[1,326,96]{1,2,0:T(8,128)S(1)}, f32[1,326,96]{1,2,0:T(8,128)S(1)}, u32[]{:S(2)}, u32[]{:S(2)}) collective-permute-start(f32[1,326,96]{1,2,0:T(8,128)S(1)} %constant_dynamic-slice_fusion), channel_id=1, source_target_pairs={{0,16},{2,18},{4,20},{6,22},{8,24},{10,26},{12,28},{14,30},{16,0},... | collective-permute-start | bytes 375560 | tf_op jit(solution)/shard_map/ppermute | solution.py:134
  165.0 5.2 %collective-permute-start.9 = (f32[326,96]{0,1:T(8,128)S(1)}, f32[326,96]{0,1:T(8,128)S(1)}, u32[]{:S(2)}, u32[]{:S(2)}) collective-permute-start(f32[326,96]{0,1:T(8,128)S(1)} %add_bitcast_fusion), channel_id=1, source_target_pairs={{0,1},{1,0},{2,3},{3,2},{4,5},{5,4},{6,7},{7,6},{8,9},{9,8},{10,11... | collective-permute-start | bytes 375560 | tf_op jit(solution)/shard_map/ppermute | solution.py:90
  170.2 1.4 collective-permute-start.10

commit v4 on v3

--- a/solution.py
+++ b/solution.py
@@ -175,7 +175,7 @@
     frames = inputs.shape[1]
     rows = inputs.shape[2]
     acts = norm_act(inputs, gain_one)
-    acts_past = passed_along(acts[:, frames - 2 :], "tm", 1)
+    acts_past = norm_act(passed_along(inputs[:, frames - 2 :], "tm", 1), gain_one)
     cot_next = passed_along(cotangent[:, :2], "tm", -1)
     both = jnp.concatenate(
         [jnp.concatenate([acts_past, acts], axis=1), jnp.concatenate([cotangent, cot_next], axis=1)]

time: 175 us -> 186 us (1.063)
  local copies, waits for them, and re-layouts: 63.2 us -> 77.8 us
  waiting for transfers between devices: 38.8 us -> 35.1 us
    reshape x3, local copies, waits for them, and re-layouts: 4.87 us -> 9.92 us  [conv_rows(): stacked = jnp.transpose(kernel, (0, 1, 3, 2, 4)).reshape(-1, 3 * width)]
    ppermute x3, waiting for transfers between devices: 12.6 us -> 9.25 us  [passed_along(): return lax.ppermute(block, axis, route)]
    slice x2, local copies, waits for them, and re-layouts: 6.97 us -> 10 us  [row_patches(): pieces = [edged[:, i:i + frames, j:j + rows] for i in order for j in order]]
    dot_general x2, matrix products: 10.7 us -> 8.69 us  [kernel_grad_rows(): jnp.dot(flat, taps, precision=lax.Precision.HIGH)]
  transfers between devices with their start and end apart: 11 -> 11, of which waited for: 7 -> 7; matrix products, arithmetic and copies ran while one was open for 21% -> 26% of each run, Pallas kernels for 0% -> 0%
where the time goes in v4:
time: 186 us; the launch traced here: 184 us
  local copies, waits for them, and re-layouts  77.8 us (42%)
  waiting for transfers between devices  35.1 us (19%)
  matrix products  28 us (15%)
  other arithmetic  22.4 us (12%)
  starting transfers between devices  19.5 us (10%)
    concatenate x3, local copies, waits for them, and re-layouts, row_patches(): taps = jnp.concatenate(pieces, axis=-1)  21.1 us
    dot_general x3, matrix products, conv_rows(): out = jnp.dot(taps, stacked, precision=lax.Precision.HIGH)  19.3 us
    ppermute x3, waiting for transfers between devices, halved_across(): blocks = keep + lax.ppermute(send, ('tm', 'height'), route)  18.4 us
    slice x2, local copies, waits for them, and re-layouts, row_patches(): pieces = [edged[:, i:i + frames, j:j + rows] for i in order for j in order]  10 us
    reshape x3, local copies, waits for them, and re-layouts, conv_rows(): stacked = jnp.transpose(kernel, (0, 1, 3, 2, 4)).reshape(-1, 3 * width)  9.92 us
    ppermute x3, starting transfers between devices, halved_across(): blocks = keep + lax.ppermute(send, ('tm', 'height'), route)  9.81 us
    ppermute x3, waiting for transfers between devices, passed_along(): return lax.ppermute(block, axis, route)  9.25 us
    dot_general x2, matrix products, kernel_grad_rows(): jnp.dot(flat, taps, precision=lax.Precision.HIGH)  8.69 us
  transfers between devices with their start and end apart: 11, of which 7 were waited for; matrix products, arithmetic and copies ran while one was open for 26% of the time, Pallas kernels for 0%

profile of v4, /device:TPU:0, one launch (start us, length us, event | category | flops | bytes accessed | tf_op | source)
XLA Modules:
  0.0 184.0 jit_solution(14179025230380664180)
XLA Ops:
  1.8 4.9 %collective-permute-start = (f32[1,2,2,160,96]{4,3,2,1,0:T(8,128)S(1)}, f32[1,2,2,160,96]{4,3,2,1,0:T(8,128)S(1)}, u32[]{:S(2)}, u32[]{:S(2)}) collective-permute-start(f32[1,2,2,160,96]{4,3,2,1,0:T(8,128)S(1)} %slice.192), channel_id=1, source_target_pairs={{0,4},{4,8},{8,12},{12,16},{16,20},{20,24},{24,28},{1,5},{5,9},{9,... | collective-permute-start | bytes 737288 | tf_op jit(solution)/shard_map/ppermute | solution.py:12
  11.4 9.2 %collective-permute-done = f32[1,2,2,160,96]{4,3,2,1,0:T(8,128)S(1)} collective-permute-done((f32[1,2,2,160,96]{4,3,2,1,0:T(8,128)S(1)}, f32[1,2,2,160,96]{4,3,2,1,0:T(8,128)S(1)}, u32[]{:S(2)}, u32[]{:S(2)}) %collective-permute-start) | collective-permute-done | bytes 245792 | tf_op jit(solution)/shard_map/ppermute | solution.py:12
  23.8 2.2 %copy.28 = f32[3,3,96,3,96]{2,1,0,4,3:T(4,128)} copy(f32[3,3,96,3,96]{2,4,3,1,0:T(8,128)S(1)} %reverse_bitcast_fusion.1) | data formatting | bytes 1990656 | tf_op jit(solution)/shard_map/transpose;transpose | solution.py:53
  25.9 3.4 %reshape.194 = f32[864,288,1,1]{0,1,2,3:T(8,128)} reshape(f32[3,3,96,3,96]{2,1,0,4,3:T(4,128)} %copy.28) | data formatting | bytes 1990656 | tf_op jit(solution)/shard_map/reshape | solution.py:53
  29.3 2.2 %copy.29 = f32[3,3,96,3,96]{2,1,0,4,3:T(4,128)} copy(f32[3,3,96,3,96]{4,2,3,1,0:T(8,128)S(1)} %bitcast.124) | data formatting | bytes 1990656 | tf_op jit(solution)/shard_map/transpose | solution.py:53
  31.5 3.3 %reshape.195 = f32[864,288,1,1]{0,1,2,3:T(8,128)} reshape(f32[3,3,96,3,96]{2,1,0,4,3:T(4,128)} %copy.29) | data formatting | bytes 1990656 | tf_op jit(solution)/shard_map/reshape | solution.py:53
  34.9 2.2 %copy.30 = f32[3,3,96,3,96]{2,1,0,4,3:T(4,128)} copy(f32[3,3,96,3,96]{2,4,3,1,0:T(8,128)S(1)} %reverse_bitcast_fusion) | data formatting | bytes 1990656 | tf_op jit(solution)/shard_map/transpose;transpose | solution.py:53
  37.0 3.3 %reshape.196 = f32[864,288,1,1]{0,1,2,3:T(8,128)} reshape(f32[3,3,96,3,96]{2,1,0,4,3:T(4,128)} %copy.30) | data formatting | bytes 1990656 | tf_op jit(solution)/shard_map/reshape | solution.py:53
  43.8 7.4 %pad_slice_fusion = (f32[1,4,2,168,96]{4,3,2,1,0:T(8,128)}, f32[1,4,2,168,96]{4,3,2,1,0:T(8,128)}, f32[1,4,2,168,96]{4,3,2,1,0:T(8,128)}, f32[1,4,2,168,96]{4,3,...) fusion(f32[1,6,4,160,96]{4,3,2,1,0:T(8,128)} %get-tuple-element, ...), kind=kLoop, calls=%fused_computation.27 | loop fusion | bytes 12238848 | tf_op jit(solution)/shard_map/slice | solution.py:45
  51.2 7.1 %concatenate.47 = f32[1,4,2,168,864]{4,3,2,1,0:T(8,128)} concatenate(f32[1,4,2,168,96]{4,3,2,1,0:T(8,128)} %get-tuple-element.60, f32[1,4,2,168,96]{4,3,2,1,0:T(8,128)} %get-tuple-element.53, f32[1,4,2,168,96]{4,3,2,1,0:T(8,128)} %get-tuple-element.54, f32[1,4,2,168,96]{4,3,2,1,0:T(8,128)} %get-tuple-element.55, f32[1,4,2,168,96]{4,3,2,1,0:T(8,128)} %get-tuple-element.56, ...), dimensions={4} | concatenate | bytes 9289728 | tf_op jit(solution)/shard_map/concatenate | solution.py:46
  58.3 6.2 %fusion.11 = f32[1,4,2,168,288]{4,3,2,1,0:T(8,128)S(1)} fusion(f32[1,4,2,168,864]{4,3,2,1,0:T(8,128)} %concatenate.47, f32[864,288,1,1]{0,1,2,3:T(8,128)S(1)} %copy-done.5), kind=kOutput, calls=%fused_computation.25 | convolution fusion | flops 2006581248 | bytes 7188480 | tf_op jit(solution)/shard_map/dot_general | solution.py:54
  65.6 6.9 %concatenate.46 = f32[1,4,2,168,864]{4,3,2,1,0:T(8,128)} concatenate(f32[1,4,2,168,96]{4,3,2,1,0:T(8,128)S(1)} %copy-done.8, f32[1,4,2,168,96]{4,3,2,1,0:T(8,128)} %get-tuple-element.77, f32[1,4,2,168,96]{4,3,2,1,0:T(8,128)} %get-tuple-element.76, f32[1,4,2,168,96]{4,3,2,1,0:T(8,128)} %get-tuple-element.75, f32[1,4,2,168,96]{4,3,2,1,0:T(8,128)} %get-tuple-element.74, ...), dimensions={4} | concatenate | bytes 9289728 | tf_op jit(solution)/shard_map/concatenate | solution.py:46
  72.5 6.8 %fusion.8 = f32[1,4,2,168,288]{4,3,2,1,0:T(8,128)S(1)} fusion(f32[1,4,2,168,864]{4,3,2,1,0:T(8,128)} %concatenate.46, f32[864,288,1,1]{0,1,2,3:T(8,128)} %reshape.194), kind=kOutput, calls=%fused_computation.24 | convolution fusion | flops 2006581248 | bytes 7188480 | tf_op jit(solution)/shard_map/dot_general | solution.py:54
  84.5 3.3 %fusion.48 = f32[288,864]{1,0:T(8,128)S(1)} fusion(f32[288,1344]{0,1:T(8,128)S(1)} %bitcast.121, f32[1344,864]{1,0:T(8,128)S(1)} %bitcast.118), kind=kOutput, calls=%fused_computation.129 | convolution fusion | flops 2006581248 | bytes 7188480 | tf_op jit(solution)/shard_map/dot_general | solution.py:69
  89.9 3.6 %copy.31 = f32[3,3,3,96,96]{4,3,2,1,0:T(8,128)} copy(f32[3,3,3,96,96]{3,1,0,4,2:T(4,128)} %bitcast.122) | data formatting | bytes 1990656 | tf_op jit(solution)/shard_map/transpose | solution.py:76
  96.4 2.5 %select_maximum_fusion = f32[1,4,2,168,288]{4,3,2,1,0:T(8,128)S(1)} fusion(f32[1,4,2,160,96]{4,3,2,1,0:T(8,128)} %get-tuple-element.63), kind=kLoop, calls=%fused_computation.12 | loop fusion | flops 3870720 | bytes 2039808 | tf_op jit(solution)/shard_map/concatenate | solution.py:61
  100.8 5.4 %fusion.49 = f32[288,864]{1,0:T(8,128)S(1)} fusion(f32[288,1344]{0,1:T(8,128)S(1)} %bitcast.120, f32[1344,864]{1,0:T(8,128)} %bitcast.115), kind=kOutput, calls=%fused_computation.130 | convolution fusion | flops 2006581248 | bytes 7188480 | tf_op jit(solution)/shard_map/dot_general | solution.py:69
  108.4 2.7 %copy.32 = f32[3,3,3,96,96]{4,3,2,1,0:T(8,128)} copy(f32[3,3,3,96,96]{4,1,0,3,2:T(4,128)} %bitcast.123) | data formatting | bytes 1990656 | tf_op jit(solution)/shard_map/transpose | solution.py:81
  116.4 2.6 %fusion.45 = (f32[1,4,2,168,96]{4,3,2,1,0:T(8,128)}, f32[1,4,2,168,96]{4,3,2,1,0:T(8,128)}, f32[1,4,2,168,96]{4,3,2,1,0:T(8,128)}, f32[1,4,2,168,96]{4,3,2,1,0:T...) fusion(f32[1,6,4,168,96]{4,3,2,1,0:T(8,128)S(1)} %select_maximu, ...), kind=kLoop, calls=%fused_computation.126 | loop fusion | bytes 9289728 | tf_op jit(solution)/shard_map/slice | solution.py:45
  119.0 7.1 %concatenate.50 = f32[1,4,2,168,864]{4,3,2,1,0:T(8,128)} concatenate(f32[1,4,2,168,96]{4,3,2,1,0:T(8,128)} %get-tuple-element.42, f32[1,4,2,168,96]{4,3,2,1,0:T(8,128)} %get-tuple-element.41, f32[1,4,2,168,96]{4,3,2,1,0:T(8,128)} %get-tuple-element.40, f32[1,4,2,168,96]{4,3,2,1,0:T(8,128)} %get-tuple-element.39, f32[1,4,2,168,96]{4,3,2,1,0:T(8,128)} %get-tuple-element.38, ...), dimensions={4} | concatenate | bytes 9289728 | tf_op jit(solution)/shard_map/concatenate | solution.py:46
  126.1 6.2 %fusion.14 = f32[1,4,2,168,288]{4,3,2,1,0:T(8,128)S(1)} fusion(f32[1,4,2,168,864]{4,3,2,1,0:T(8,128)} %concatenate.50, f32[864,288,1,1]{0,1,2,3:T(8,128)S(1)} %copy-done.4), kind=kOutput, calls=%fused_computation.26 | convolution fusion | flops 2006581248 | bytes 7188480 | tf_op jit(solution)/shard_map/dot_general | solution.py:54
  134.8 3.3 %maximum_multiply_fusion = f32[8,652,96]{1,2,0:T(8,128)} fusion(f32[8,4,96]{1,2,0:T(8,128)S(1)} %broadcast_in_dim.14, f32[8,324,96]{1,2,0:T(8,128)} %copy.35, f32[8,324,96]{1,2,0:T(8,128)S(1)} %copy-done.3), kind=kLoop, calls=%fused_computation.11 | loop fusion | flops 1502208 | bytes 4005888 | tf_op jit(solution)/shard_map/mul | solution.py:231
  138.1 3.3 %mul.241 = f32[8,2,326,96]{2,1,3,0:T(2,128)S(1)} reshape(f32[8,652,96]{1,2,0:T(8,128)} %maximum_multiply_fusion) | data formatting | bytes 4005888 | tf_op jit(solution)/shard_map/mul | solution.py:231
  141.4 2.3 %constant_dynamic-slice_fusion.2 = (f32[8,1,326,96]{2,1,3,0:T(1,128)S(1)}, f32[8,1,326,96]{2,1,3,0:T(1,128)S(1)}) fusion(f32[8,2,326,96]{2,1,3,0:T(2,128)S(1)} %mul.241, s32[]{:T(128)S(6)} %select_n.139, s32[]{:T(128)S(6)} %select_n.140), kind=kLoop, calls=%fused_computation.123 | loop fusion | bytes 4005896 | tf_op jit(solution)/shard_map/dynamic-slice.4
  144.3 2.5 %collective-permute-done.5 = f32[1,8,326,96]{2,3,1,0:T(8,128)S(1)} collective-permute-done((f32[1,8,326,96]{2,3,1,0:T(8,128)S(1)}, f32[1,8,326,96]{2,3,1,0:T(8,128)S(1)}, u32[]{:S(2)}, u32[]{:S(2)}) %collective-permute-start.5) | collective-permute-done | bytes 1001504 | tf_op jit(solution)/shard_map/ppermute | solution.py:90
  147.3 3.2 %collective-permute-start.6 = (f32[4,326,96]{1,2,0:T(8,128)S(1)}, f32[4,326,96]{1,2,0:T(8,128)S(1)}, u32[]{:S(2)}, u32[]{:S(2)}) collective-permute-start(f32[4,326,96]{1,2,0:T(8,128)S(1)} %dynamic-slice_bitcast_fusion), channel_id=1, source_target_pairs={{0,4},{2,10},{4,0},{6,14},{8,12},{10,2},{12,8},{14,6},{16,20},{18,... | collective-permute-start | bytes 1502216 | tf_op jit(solution)/shard_map/ppermute | solution.py:134
  150.5 7.9 %collective-permute-done.6 = f32[4,326,96]{1,2,0:T(8,128)S(1)} collective-permute-done((f32[4,326,96]{1,2,0:T(8,128)S(1)}, f32[4,326,96]{1,2,0:T(8,128)S(1)}, u32[]{:S(2)}, u32[]{:S(2)}) %collective-permute-start.6) | collective-permute-done | bytes 500768 | tf_op jit(solution)/shard_map/ppermute | solution.py:134
  158.4 3.5 %collective-permute-start.7 = (f32[2,326,96]{1,2,0:T(8,128)S(1)}, f32[2,326,96]{1,2,0:T(8,128)S(1)}, u32[]{:S(2)}, u32[]{:S(2)}) collective-permute-start(f32[2,326,96]{1,2,0:T(8,128)S(1)} %dynamic-slice_bitcast_fusion.1), channel_id=1, source_target_pairs={{0,8},{2,6},{4,12},{6,2},{8,0},{10,14},{12,4},{14,10},{16,24},{18,... | collective-permute-start | bytes 751112 | tf_op jit(solution)/shard_map/ppermute | solution.py:134
  162.0 4.7 %collective-permute-done.7 = f32[2,326,96]{1,2,0:T(8,128)S(1)} collective-permute-done((f32[2,326,96]{1,2,0:T(8,128)S(1)}, f32[2,326,96]{1,2,0:T(8,128)S(1)}, u32[]{:S(2)}, u32[]{:S(2)}) %collective-permute-start.7) | collective-permute-done | bytes 250400 | tf_op jit(solution)/shard_map/ppermute | solution.py:134
  166.7 3.1 %collective-permute-start.8 = (f32[1,326,96]{1,2,0:T(8,128)S(1)}, f32[1,326,96]{1,2,0:T(8,128)S(1)}, u32[]{:S(2)}, u32[]{:S(2)}) collective-permute-start(f32[1,326,96]{1,2,0:T(8,128)S(1)} %constant_dynamic-slice_fusion), channel_id=1, source_target_pairs={{0,16},{2,18},{4,20},{6,22},{8,24},{10,26},{12,28},{14,30},{16,0},... | collective-permute-start | bytes 375560 | tf_op jit(solution)/shard_map/ppermute | solution.py:134
  169.8 5.8 %collective-permute-done.8 = f32[1,326,96]{1,2,0:T(8,128)S(1)} collective-permute-done((f32[1,326,96]{1,2,0:T(8,128)S(1)}, f32[1,326,96]{1,2,0:T(8,128)S(1)}, u32[]{:S(2)}, u32[]{:S(2)}) %collective-permute-start.8) | collective-permute-done | bytes 125216 | tf_op jit(solution)/shard_map/ppermute | solution.py:134
  177.3 3.6 %collective-permute-done.9 = f32[326,96]{0,1:T(8,128)S(1)} collective-permute-done((f32[326,96]{0,1:T(8,128)S(1)}, f32[326,96]{0,1:T(8,128)S(1)}, u32[]{:S(2)}, u32[]{:S(2)}) %collective-permute-start.9) | collective-permute-done | bytes 125216 | tf_op jit(solution)/shard_map/ppermute | solution.py:90
  (106 shorter events, 41.2 us)
Async XLA Ops:
  0.6 9.8 %copy-start = (f32[1,4,2,160,96]{4,3,2,1,0:T(8,128)S(1)}, f32[1,4,2,160,96]{4,3,2,1,0:T(8,128)}, u32[]{:S(2)}) copy-start(f32[1,4,2,160,96]{4,3,2,1,0:T(8,128)} %param.7) | copy-start | bytes 1474564
  0.6 21.2 %copy-start.1 = (f32[1,4,2,160,96]{4,3,2,1,0:T(8,128)S(1)}, f32[1,4,2,160,96]{4,3,2,1,0:T(8,128)}, u32[]{:S(2)}) copy-start(f32[1,4,2,160,96]{4,3,2,1,0:T(8,128)} %param.13) | copy-start | bytes 1474564
  0.7 20.2 %copy-start.12 = (f32[96]{0:T(128)S(1)}, f32[96]{0:T(128)}, u32[]{:S(2)}) copy-start(f32[96]{0:T(128)} %param.10) | copy-start | bytes 1156
  1.8 18.9 %collective-permute-start = (f32[1,2,2,160,96]{4,3,2,1,0:T(8,128)S(1)}, f32[1,2,2,160,96]{4,3,2,1,0:T(8,128)S(1)}, u32[]{:S(2)}, u32[]{:S(2)}) collective-permute-start(f32[1,2,2,160,96]{4,3,2,1,0:T(8,128)S(1)} %slice.192), channel_id=1, source_target_pairs={{0,4},{4,8},{8,12},{12,16},{16,20},{20,24},{24,28},{1,5},{5,9},{9,... | collective-permute-start | bytes 737288 | tf_op jit(solution)/shard_map/ppermute | solution.py:12
  7.7 13.4 %collective-permute-start.1 = (f32[1,2,2,160,96]{4,3,2,1,0:T(8,128)S(1)}, f32[1,2,2,160,96]{4,3,2,1,0:T(8,128)S(1)}, u32[]{:S(2)}, u32[]{:S(2)}) collective-permute-start(f32[1,2,2,160,96]{4,3,2,1,0:T(8,128)S(1)} %slice.193), channel_id=1, source_target_pairs={{4,0},{8,4},{12,8},{16,12},{20,16},{24,20},{28,24},{5,1},{9,5},{13... | collective-permute-start | bytes 737288 | tf_op jit(solution)/shard_map/ppermute | solution.py:12
  21.0 2.0 %copy-start.6 = (f32[1,2,2,160,96]{4,3,2,1,0:T(8,128)}, f32[1,2,2,160,96]{4,3,2,1,0:T(8,128)S(1)}, u32[]{:S(2)}) copy-start(f32[1,2,2,160,96]{4,3,2,1,0:T(8,128)S(1)} %divide_multiply_fusion) | copy-start | bytes 737284
  21.1 0.8 copy-start.10
  22.0 1.7 copy-start.9
  23.1 17.2 %collective-permute-start.2 = (f32[2,6,1,160,96]{4,3,2,1,0:T(8,128)}, f32[2,6,1,160,96]{4,3,2,1,0:T(8,128)}, u32[]{:S(2)}, u32[]{:S(2)}) collective-permute-start(f32[2,6,1,160,96]{4,3,2,1,0:T(8,128)} %slice_select_fusion), channel_id=1, source_target_pairs={{0,2},{2,0},{1,3},{3,1},{4,6},{6,4},{5,7},{7,5},{8,10},{10,8},{9,1... | collective-permute-start | bytes 2211848 | tf_op jit(solution)/shard_map/ppermute | solution.py:22
  25.9 3.4 %copy-start.2 = (f32[3,3,3,96,96]{4,3,2,1,0:T(8,128)S(1)}, f32[3,3,3,96,96]{4,3,2,1,0:T(8,128)}, u32[]{:S(2)}) copy-start(f32[3,3,3,96,96]{4,3,2,1,0:T(8,128)} %param.8) | copy-start | bytes 2985988
  40.3 1.5 copy-start.7
  40.3 1.5 copy-start.11
  51.2 7.1 %copy-start.5 = (f32[864,288,1,1]{0,1,2,3:T(8,128)S(1)}, f32[864,288,1,1]{0,1,2,3:T(8,128)}, u32[]{:S(2)}) copy-start(f32[864,288,1,1]{0,1,2,3:T(8,128)} %reshape.195) | copy-start | bytes 2985988
  58.3 6.2 %copy-start.14 = (f32[96]{0:T(128)S(1)}, f32[96]{0:T(128)}, u32[]{:S(2)}) copy-start(f32[96]{0:T(128)} %param.9) | copy-start | bytes 1156
  64.5 1.1 copy-start.8
  72.5 6.9 %copy-start.13 = (f32[96]{0:T(128)S(1)}, f32[96]{0:T(128)}, u32[]{:S(2)}) copy-start(f32[96]{0:T(128)} %param.12) | copy-start | bytes 1156
  72.5 12.0 %slice-start = ((s8[4816896]{0:T(1024)(128)(4,1)}), s8[4194304]{0:T(1024)(128)(4,1)S(1)}, s32[]{:S(2)}) async-start(s8[4816896]{0:T(1024)(128)(4,1)} %bitcast.116), calls=%async_computation | async-start | bytes 8388608
  79.4 5.2 %slice-start.1 = ((s8[4816896]{0:T(1024)(128)(4,1)}), s8[622592]{0:T(1024)(128)(4,1)S(1)}, s32[]{:S(2)}) async-start(s8[4816896]{0:T(1024)(128)(4,1)} %bitcast.116), calls=%async_computation.1 | async-start | bytes 1245184
  83.2 15.7 %collective-permute-start.3 = (f32[1,2,2,160,96]{4,3,2,1,0:T(8,128)}, f32[1,2,2,160,96]{4,3,2,1,0:T(8,128)}, u32[]{:S(2)}, u32[]{:S(2)}) collective-permute-start(f32[1,2,2,160,96]{4,3,2,1,0:T(8,128)} %slice.266), channel_id=1, source_target_pairs={{4,0},{8,4},{12,8},{16,12},{20,16},{24,20},{28,24},{5,1},{9,5},{13... | collective-permute-start | bytes 737288 | tf_op jit(solution)/shard_map/ppermute | solution.py:12
  100.8 13.2 %collective-permute-start.4 = (f32[1,6,1,160,96]{4,3,2,1,0:T(8,128)}, f32[1,6,1,160,96]{4,3,2,1,0:T(8,128)}, u32[]{:S(2)}, u32[]{:S(2)}) collective-permute-start(f32[1,6,1,160,96]{4,3,2,1,0:T(8,128)} %fusion.29), channel_id=1, source_target_pairs={{0,2},{2,0},{1,3},{3,1},{4,6},{6,4},{5,7},{7,5},{8,10},{10,8},{9,1... | collective-permute-start | bytes 1105928 | tf_op jit(solution)/shard_map/ppermute | solution.py:22
  119.0 7.1 %copy-start.4 = (f32[864,288,1,1]{0,1,2,3:T(8,128)S(1)}, f32[864,288,1,1]{0,1,2,3:T(8,128)}, u32[]{:S(2)}) copy-start(f32[864,288,1,1]{0,1,2,3:T(8,128)} %reshape.196) | copy-start | bytes 2985988
  133.3 1.4 copy-start.3
  143.7 3.0 %collective-permute-start.5 = (f32[1,8,326,96]{2,3,1,0:T(8,128)S(1)}, f32[1,8,326,96]{2,3,1,0:T(8,128)S(1)}, u32[]{:S(2)}, u32[]{:S(2)}) collective-permute-start(f32[1,8,326,96]{2,3,1,0:T(8,128)S(1)} %bitcast.128), channel_id=1, source_target_pairs={{0,2},{2,0},{1,3},{3,1},{4,6},{6,4},{5,7},{7,5},{8,10},{10,8},{9,1... | collective-permute-start | bytes 3004424 | tf_op jit(solution)/shard_map/ppermute | solution.py:90
  147.3 11.0 %collective-permute-start.6 = (f32[4,326,96]{1,2,0:T(8,128)S(1)}, f32[4,326,96]{1,2,0:T(8,128)S(1)}, u32[]{:S(2)}, u32[]{:S(2)}) collective-permute-start(f32[4,326,96]{1,2,0:T(8,128)S(1)} %dynamic-slice_bitcast_fusion), channel_id=1, source_target_pairs={{0,4},{2,10},{4,0},{6,14},{8,12},{10,2},{12,8},{14,6},{16,20},{18,... | collective-permute-start | bytes 1502216 | tf_op jit(solution)/shard_map/ppermute | solution.py:134
  158.4 8.2 %collective-permute-start.7 = (f32[2,326,96]{1,2,0:T(8,128)S(1)}, f32[2,326,96]{1,2,0:T(8,128)S(1)}, u32[]{:S(2)}, u32[]{:S(2)}) collective-permute-start(f32[2,326,96]{1,2,0:T(8,128)S(1)} %dynamic-slice_bitcast_fusion.1), channel_id=1, source_target_pairs={{0,8},{2,6},{4,12},{6,2},{8,0},{10,14},{12,4},{14,10},{16,24},{18,... | collective-permute-start | bytes 751112 | tf_op jit(solution)/shard_map/ppermute | solution.py:134
  166.7 8.9 %collective-permute-start.8 = (f32[1,326,96]{1,2,0:T(8,128)S(1)}, f32[1,326,96]{1,2,0:T(8,128)S(1)}, u32[]{:S(2)}, u32[]{:S(2)}) collective-permute-start(f32[1,326,96]{1,2,0:T(8,128)S(1)} %constant_dynamic-slice_fusion), channel_id=1, source_target_pairs={{0,16},{2,18},{4,20},{6,22},{8,24},{10,26},{12,28},{14,30},{16,0},... | collective-permute-start | bytes 375560 | tf_op jit(solution)/shard_map/ppermute | solution.py:134
  175.7 5.2 %collective-permute-start.9 = (f32[326,96]{0,1:T(8,128)S(1)}, f32[326,96]{0,1:T(8,128)S(1)}, u32[]{:S(2)}, u32[]{:S(2)}) collective-permute-start(f32[326,96]{0,1:T(8,128)S(1)} %add_bitcast_fusion), channel_id=1, source_target_pairs={{0,1},{1,0},{2,3},{3,2},{4,5},{5,4},{6,7},{7,6},{8,9},{9,8},{10,11... | collective-permute-start | bytes 375560 | tf_op jit(solution)/shard_map/ppermute | solution.py:90
  180.9 1.4 collective-permute-start.10

commit v5 on v3

--- a/solution.py
+++ b/solution.py
@@ -90,20 +90,21 @@
     return lax.ppermute(block, axis, [(i, i ^ bit) for i in range(count)])
 
 
-def halved(blocks, axis):
+def halved(blocks, axis, dim=0):
     count = lax.axis_size(axis)
     if count & (count - 1):
-        return lax.psum_scatter(blocks, axis, scatter_dimension=0)
+        return lax.psum_scatter(blocks, axis, scatter_dimension=dim)
     me = lax.axis_index(axis)
     bit = 1
     while bit < count:
         mine = (me // bit) % 2
-        pairs = blocks.reshape((blocks.shape[0] // 2, 2) + blocks.shape[1:])
-        keep = lax.dynamic_index_in_dim(pairs, mine, axis=1, keepdims=False)
-        send = lax.dynamic_index_in_dim(pairs, 1 - mine, axis=1, keepdims=False)
+        shape = blocks.shape
+        pairs = blocks.reshape(shape[:dim] + (shape[dim] // 2, 2) + shape[dim + 1 :])
+        keep = lax.dynamic_index_in_dim(pairs, mine, axis=dim + 1, keepdims=False)
+        send = lax.dynamic_index_in_dim(pairs, 1 - mine, axis=dim + 1, keepdims=False)
         blocks = keep + exchanged(send, axis, bit)
         bit *= 2
-    return blocks[0]
+    return lax.index_in_dim(blocks, 0, dim, keepdims=False)
 
 
 def swapped_low(t):
@@ -166,8 +167,8 @@
     split = lax.axis_size("height")
     width = -(-size // split)
     blocks = jnp.pad(blocks, ((0, 0), (0, width * split - size), (0, 0)))
-    blocks = jnp.swapaxes(blocks.reshape(parts, split, width, channels), 0, 1)
-    block = halved_across(halved(blocks, "height"))
+    blocks = blocks.reshape(parts, split, width, channels)
+    block = halved_across(halved(blocks, "height", 1))
     return gathered(summed(block, "batch"), "height")[:size]
 
 

time: 175 us -> 175 us (level)
    another operation x1 -> x0, local copies, waits for them, and re-layouts: 2.28 us -> none
    dynamic_slice x0 -> x1, local copies, waits for them, and re-layouts: none -> 2.28 us  [halved(): keep = lax.dynamic_index_in_dim(pairs, mine, axis=dim + 1, keepdims=False)]
where the time goes in v5:
time: 175 us; the launch traced here: 173 us
  local copies, waits for them, and re-layouts  63.2 us (36%)
  waiting for transfers between devices  38.8 us (22%)
  matrix products  29.7 us (17%)
  other arithmetic  20.8 us (12%)
  starting transfers between devices  19.5 us (11%)
    concatenate x3, local copies, waits for them, and re-layouts, row_patches(): taps = jnp.concatenate(pieces, axis=-1)  21.1 us
    dot_general x3, matrix products, conv_rows(): out = jnp.dot(taps, stacked, precision=lax.Precision.HIGH)  19 us
    ppermute x3, waiting for transfers between devices, halved_across(): blocks = keep + lax.ppermute(send, ('tm', 'height'), route)  18.8 us
    ppermute x3, waiting for transfers between devices, passed_along(): return lax.ppermute(block, axis, route)  12.6 us
    dot_general x2, matrix products, kernel_grad_rows(): jnp.dot(flat, taps, precision=lax.Precision.HIGH)  10.7 us
    ppermute x3, starting transfers between devices, halved_across(): blocks = keep + lax.ppermute(send, ('tm', 'height'), route)  9.81 us
    ppermute x3, starting transfers between devices, passed_along(): return lax.ppermute(block, axis, route)  7.46 us
    ppermute x3, waiting for transfers between devices, exchanged(): return lax.ppermute(block, axis, [(i, i ^ bit) for i in range(count)])  7.45 us
  transfers between devices with their start and end apart: 11, of which 7 were waited for; matrix products, arithmetic and copies ran while one was open for 21% of the time, Pallas kernels for 0%

profile of v5, /device:TPU:0, one launch (start us, length us, event | category | flops | bytes accessed | tf_op | source)
XLA Modules:
  0.0 173.3 jit_solution(17471975105134681846)
XLA Ops:
  3.6 4.9 %collective-permute-start = (f32[1,2,2,160,96]{4,3,2,1,0:T(8,128)S(1)}, f32[1,2,2,160,96]{4,3,2,1,0:T(8,128)S(1)}, u32[]{:S(2)}, u32[]{:S(2)}) collective-permute-start(f32[1,2,2,160,96]{4,3,2,1,0:T(8,128)S(1)} %slice.256), channel_id=1, source_target_pairs={{0,4},{4,8},{8,12},{12,16},{16,20},{20,24},{24,28},{1,5},{5,9},{9,... | collective-permute-start | bytes 737288 | tf_op jit(solution)/shard_map/ppermute | solution.py:12
  9.8 12.6 %collective-permute-done = f32[1,2,2,160,96]{4,3,2,1,0:T(8,128)S(1)} collective-permute-done((f32[1,2,2,160,96]{4,3,2,1,0:T(8,128)S(1)}, f32[1,2,2,160,96]{4,3,2,1,0:T(8,128)S(1)}, u32[]{:S(2)}, u32[]{:S(2)}) %collective-permute-start) | collective-permute-done | bytes 245792 | tf_op jit(solution)/shard_map/ppermute | solution.py:12
  26.0 1.6 reshape.180
  27.6 2.6 %copy.38 = f32[3,3,96,3,96]{2,1,0,4,3:T(4,128)S(1)} copy(f32[3,3,96,3,96]{4,2,3,1,0:T(8,128)} %bitcast.126) | data formatting | bytes 1990656 | tf_op jit(solution)/shard_map/transpose | solution.py:53
  30.2 1.6 reshape.181
  34.2 1.6 reshape.182
  37.9 4.5 %pad_slice_fusion = (f32[1,4,2,168,96]{4,3,2,1,0:T(8,128)}, f32[1,4,2,168,96]{4,3,2,1,0:T(8,128)}, f32[1,4,2,168,96]{4,3,2,1,0:T(8,128)}, f32[1,4,2,168,96]{4,3,...) fusion(f32[1,6,4,160,96]{4,3,2,1,0:T(8,128)S(1)} %get-tuple-ele, ...), kind=kLoop, calls=%fused_computation.27 | loop fusion | bytes 12238848 | tf_op jit(solution)/shard_map/slice | solution.py:45
  42.5 7.1 %concatenate.47 = f32[1,4,2,168,864]{4,3,2,1,0:T(8,128)} concatenate(f32[1,4,2,168,96]{4,3,2,1,0:T(8,128)} %get-tuple-element.60, f32[1,4,2,168,96]{4,3,2,1,0:T(8,128)} %get-tuple-element.53, f32[1,4,2,168,96]{4,3,2,1,0:T(8,128)} %get-tuple-element.54, f32[1,4,2,168,96]{4,3,2,1,0:T(8,128)} %get-tuple-element.55, f32[1,4,2,168,96]{4,3,2,1,0:T(8,128)} %get-tuple-element.56, ...), dimensions={4} | concatenate | bytes 9289728 | tf_op jit(solution)/shard_map/concatenate | solution.py:46
  49.5 6.2 %fusion.11 = f32[1,4,2,168,288]{4,3,2,1,0:T(8,128)S(1)} fusion(f32[1,4,2,168,864]{4,3,2,1,0:T(8,128)} %concatenate.47, f32[864,288,1,1]{0,1,2,3:T(8,128)S(1)} %copy-done.5), kind=kOutput, calls=%fused_computation.25 | convolution fusion | flops 2006581248 | bytes 7188480 | tf_op jit(solution)/shard_map/dot_general | solution.py:54
  56.5 7.1 %concatenate.46 = f32[1,4,2,168,864]{4,3,2,1,0:T(8,128)} concatenate(f32[1,4,2,168,96]{4,3,2,1,0:T(8,128)} %get-tuple-element.70, f32[1,4,2,168,96]{4,3,2,1,0:T(8,128)} %get-tuple-element.77, f32[1,4,2,168,96]{4,3,2,1,0:T(8,128)} %get-tuple-element.76, f32[1,4,2,168,96]{4,3,2,1,0:T(8,128)} %get-tuple-element.75, f32[1,4,2,168,96]{4,3,2,1,0:T(8,128)} %get-tuple-element.74, ...), dimensions={4} | concatenate | bytes 9289728 | tf_op jit(solution)/shard_map/concatenate | solution.py:46
  63.6 6.5 %fusion.8 = f32[1,4,2,168,288]{4,3,2,1,0:T(8,128)S(1)} fusion(f32[1,4,2,168,864]{4,3,2,1,0:T(8,128)} %concatenate.46, f32[864,288,1,1]{0,1,2,3:T(8,128)S(1)} %copy-done.4), kind=kOutput, calls=%fused_computation.24 | convolution fusion | flops 2006581248 | bytes 7188480 | tf_op jit(solution)/shard_map/dot_general | solution.py:54
  70.2 1.7 %multiply_reduce_fusion = (f32[96]{0:T(128)S(1)}, f32[4,2,160]{2,1,0:T(2,128)S(1)}, f32[1,4,2,160,96]{4,3,2,1,0:T(8,128)S(1)}, f32[1,4,2,160,96]{4,3,2,1,0:T(8,128)}) fusion(f32[1,4,2,160,96]{4,3,2,1,0:T(8,128)S(1)} %get-tuple-element.29, f32[4,2,160]{2,1,0:T(2,128)S(1)} %fusion.39, f32[96]{0:T(128)S(1)} %copy-done.11, f32[1,4,2,168,288]{4,3,2,1,0:T(8,128)S(1)} %fusion.8), kind=kLoop, calls=%fused_computation.72 | loop fusion | flops 2333344 | bytes 2960128 | tf_op jit(solution)/shard_map/transpose(jvp())/reduce_sum | solution.py:37
  75.4 4.3 %fusion.48 = f32[288,864]{1,0:T(8,128)} fusion(f32[288,1344]{0,1:T(8,128)S(1)} %bitcast.123, f32[1344,864]{1,0:T(8,128)S(1)} %bitcast.120), kind=kOutput, calls=%fused_computation.126 | convolution fusion | flops 2006581248 | bytes 7188480 | tf_op jit(solution)/shard_map/dot_general | solution.py:69
  79.6 2.5 %reshape.175 = f32[3,96,3,3,96]{4,3,2,1,0:T(4,128)S(1)} reshape(f32[288,864]{1,0:T(8,128)} %fusion.48) | data formatting | bytes 1990656 | tf_op jit(solution)/shard_map/reshape | solution.py:70
  82.2 2.2 %copy.40 = f32[3,3,3,96,96]{4,3,2,1,0:T(8,128)} copy(f32[3,3,3,96,96]{3,1,0,4,2:T(4,128)S(1)} %bitcast.124) | data formatting | bytes 1990656 | tf_op jit(solution)/shard_map/transpose | solution.py:76
  88.2 1.8 %fusion.29 = f32[1,6,1,160,96]{4,3,2,1,0:T(8,128)} fusion(f32[1,4,2,160,96]{4,3,2,1,0:T(8,128)S(1)} %get-tuple-element.25, f32[1,2,2,160,96]{4,3,2,1,0:T(8,128)} %collective-permute-done.3, pred[]{:T(512)S(6)} %eq.20), kind=kLoop, calls=%fused_computation.85 | loop fusion | flops 276480 | bytes 1105921 | tf_op jit(solution)/shard_map/jit(_where)/select_n | solution.py:22
  90.0 6.4 %fusion.49 = f32[288,864]{1,0:T(8,128)} fusion(f32[288,1344]{0,1:T(8,128)S(1)} %bitcast.122, f32[1344,864]{1,0:T(8,128)} %bitcast.117), kind=kOutput, calls=%fused_computation.127 | convolution fusion | flops 2006581248 | bytes 7188480 | tf_op jit(solution)/shard_map/dot_general | solution.py:69
  96.4 2.5 %reshape.178 = f32[3,96,3,3,96]{4,3,2,1,0:T(4,128)S(1)} reshape(f32[288,864]{1,0:T(8,128)} %fusion.49) | data formatting | bytes 1990656 | tf_op jit(solution)/shard_map/reshape | solution.py:70
  105.4 2.5 %fusion.45 = (f32[1,4,2,168,96]{4,3,2,1,0:T(8,128)S(1)}, f32[1,4,2,168,96]{4,3,2,1,0:T(8,128)}, f32[1,4,2,168,96]{4,3,2,1,0:T(8,128)}, f32[1,4,2,168,96]{4,3,2,1...) fusion(f32[1,6,4,168,96]{4,3,2,1,0:T(8,128)S(1)} %select_maximu, ...), kind=kLoop, calls=%fused_computation.123 | loop fusion | bytes 9289728 | tf_op jit(solution)/shard_map/slice | solution.py:45
  107.9 7.0 %concatenate.50 = f32[1,4,2,168,864]{4,3,2,1,0:T(8,128)} concatenate(f32[1,4,2,168,96]{4,3,2,1,0:T(8,128)} %get-tuple-element.42, f32[1,4,2,168,96]{4,3,2,1,0:T(8,128)} %get-tuple-element.41, f32[1,4,2,168,96]{4,3,2,1,0:T(8,128)} %get-tuple-element.40, f32[1,4,2,168,96]{4,3,2,1,0:T(8,128)} %get-tuple-element.39, f32[1,4,2,168,96]{4,3,2,1,0:T(8,128)} %get-tuple-element.38, ...), dimensions={4} | concatenate | bytes 9289728 | tf_op jit(solution)/shard_map/concatenate | solution.py:46
  115.0 6.3 %fusion.14 = f32[1,4,2,168,288]{4,3,2,1,0:T(8,128)S(1)} fusion(f32[1,4,2,168,864]{4,3,2,1,0:T(8,128)} %concatenate.50, f32[864,288,1,1]{0,1,2,3:T(8,128)S(1)} %copy-done.3), kind=kOutput, calls=%fused_computation.26 | convolution fusion | flops 2006581248 | bytes 7188480 | tf_op jit(solution)/shard_map/dot_general | solution.py:54
  123.7 3.3 %maximum_multiply_fusion = f32[8,652,96]{1,2,0:T(8,128)} fusion(f32[8,4,96]{1,2,0:T(8,128)S(1)} %broadcast_in_dim.14, f32[8,324,96]{1,2,0:T(8,128)} %copy.44, f32[8,324,96]{1,2,0:T(8,128)S(1)} %copy-done.2), kind=kLoop, calls=%fused_computation.11 | loop fusion | flops 1502208 | bytes 4005888 | tf_op jit(solution)/shard_map/mul | solution.py:232
  127.0 3.3 %mul.218 = f32[8,1,2,326,96]{3,2,4,0,1:T(2,128)S(1)} reshape(f32[8,652,96]{1,2,0:T(8,128)} %maximum_multiply_fusion) | data formatting | bytes 4005888 | tf_op jit(solution)/shard_map/mul | solution.py:232
  130.3 2.3 %constant_dynamic-slice_fusion.2 = (f32[8,1,1,326,96]{3,2,4,0,1:T(1,128)S(1)}, f32[8,1,1,326,96]{3,2,4,0,1:T(1,128)S(1)}) fusion(f32[8,1,2,326,96]{3,2,4,0,1:T(2,128)S(1)} %mul.218, s32[]{:T(128)S(6)} %select_n.139, s32[]{:T(128)S(6)} %select_n.140), kind=kLoop, calls=%fused_computation.120 | loop fusion | bytes 4005896 | tf_op jit(solution)/shard_map/jit(dynamic_index_in_dim)/dynamic_slice | solution.py:103
  133.2 2.5 %collective-permute-done.5 = f32[8,1,326,96]{2,3,1,0:T(8,128)S(1)} collective-permute-done((f32[8,1,326,96]{2,3,1,0:T(8,128)S(1)}, f32[8,1,326,96]{2,3,1,0:T(8,128)S(1)}, u32[]{:S(2)}, u32[]{:S(2)}) %collective-permute-start.5) | collective-permute-done | bytes 1001504 | tf_op jit(solution)/shard_map/ppermute | solution.py:90
  136.2 3.2 %collective-permute-start.6 = (f32[4,326,96]{1,2,0:T(8,128)S(1)}, f32[4,326,96]{1,2,0:T(8,128)S(1)}, u32[]{:S(2)}, u32[]{:S(2)}) collective-permute-start(f32[4,326,96]{1,2,0:T(8,128)S(1)} %dynamic-slice_bitcast_fusion), channel_id=1, source_target_pairs={{0,4},{2,10},{4,0},{6,14},{8,12},{10,2},{12,8},{14,6},{16,20},{18,... | collective-permute-start | bytes 1502216 | tf_op jit(solution)/shard_map/ppermute | solution.py:135
  139.4 7.9 %collective-permute-done.6 = f32[4,326,96]{1,2,0:T(8,128)S(1)} collective-permute-done((f32[4,326,96]{1,2,0:T(8,128)S(1)}, f32[4,326,96]{1,2,0:T(8,128)S(1)}, u32[]{:S(2)}, u32[]{:S(2)}) %collective-permute-start.6) | collective-permute-done | bytes 500768 | tf_op jit(solution)/shard_map/ppermute | solution.py:135
  147.3 3.5 %collective-permute-start.7 = (f32[2,326,96]{1,2,0:T(8,128)S(1)}, f32[2,326,96]{1,2,0:T(8,128)S(1)}, u32[]{:S(2)}, u32[]{:S(2)}) collective-permute-start(f32[2,326,96]{1,2,0:T(8,128)S(1)} %dynamic-slice_bitcast_fusion.1), channel_id=1, source_target_pairs={{0,8},{2,6},{4,12},{6,2},{8,0},{10,14},{12,4},{14,10},{16,24},{18,... | collective-permute-start | bytes 751112 | tf_op jit(solution)/shard_map/ppermute | solution.py:135
  150.9 4.7 %collective-permute-done.7 = f32[2,326,96]{1,2,0:T(8,128)S(1)} collective-permute-done((f32[2,326,96]{1,2,0:T(8,128)S(1)}, f32[2,326,96]{1,2,0:T(8,128)S(1)}, u32[]{:S(2)}, u32[]{:S(2)}) %collective-permute-start.7) | collective-permute-done | bytes 250400 | tf_op jit(solution)/shard_map/ppermute | solution.py:135
  155.6 3.1 %collective-permute-start.8 = (f32[1,326,96]{1,2,0:T(8,128)S(1)}, f32[1,326,96]{1,2,0:T(8,128)S(1)}, u32[]{:S(2)}, u32[]{:S(2)}) collective-permute-start(f32[1,326,96]{1,2,0:T(8,128)S(1)} %constant_dynamic-slice_fusion), channel_id=1, source_target_pairs={{0,16},{2,18},{4,20},{6,22},{8,24},{10,26},{12,28},{14,30},{16,0},... | collective-permute-start | bytes 375560 | tf_op jit(solution)/shard_map/ppermute | solution.py:135
  158.7 6.2 %collective-permute-done.8 = f32[1,326,96]{1,2,0:T(8,128)S(1)} collective-permute-done((f32[1,326,96]{1,2,0:T(8,128)S(1)}, f32[1,326,96]{1,2,0:T(8,128)S(1)}, u32[]{:S(2)}, u32[]{:S(2)}) %collective-permute-start.8) | collective-permute-done | bytes 125216 | tf_op jit(solution)/shard_map/ppermute | solution.py:135
  166.5 3.6 %collective-permute-done.9 = f32[326,96]{0,1:T(8,128)S(1)} collective-permute-done((f32[326,96]{0,1:T(8,128)S(1)}, f32[326,96]{0,1:T(8,128)S(1)}, u32[]{:S(2)}, u32[]{:S(2)}) %collective-permute-start.9) | collective-permute-done | bytes 125216 | tf_op jit(solution)/shard_map/ppermute | solution.py:90
  (99 shorter events, 34.9 us)
Async XLA Ops:
  0.6 7.8 %copy-start.1 = (f32[1,4,2,160,96]{4,3,2,1,0:T(8,128)S(1)}, f32[1,4,2,160,96]{4,3,2,1,0:T(8,128)}, u32[]{:S(2)}) copy-start(f32[1,4,2,160,96]{4,3,2,1,0:T(8,128)} %param.13) | copy-start | bytes 1474564
  3.6 18.9 %collective-permute-start = (f32[1,2,2,160,96]{4,3,2,1,0:T(8,128)S(1)}, f32[1,2,2,160,96]{4,3,2,1,0:T(8,128)S(1)}, u32[]{:S(2)}, u32[]{:S(2)}) collective-permute-start(f32[1,2,2,160,96]{4,3,2,1,0:T(8,128)S(1)} %slice.256), channel_id=1, source_target_pairs={{0,4},{4,8},{8,12},{12,16},{16,20},{20,24},{24,28},{1,5},{5,9},{9,... | collective-permute-start | bytes 737288 | tf_op jit(solution)/shard_map/ppermute | solution.py:12
  8.5 13.9 %collective-permute-start.1 = (f32[1,2,2,160,96]{4,3,2,1,0:T(8,128)S(1)}, f32[1,2,2,160,96]{4,3,2,1,0:T(8,128)S(1)}, u32[]{:S(2)}, u32[]{:S(2)}) collective-permute-start(f32[1,2,2,160,96]{4,3,2,1,0:T(8,128)S(1)} %slice.193), channel_id=1, source_target_pairs={{4,0},{8,4},{12,8},{16,12},{20,16},{24,20},{28,24},{5,1},{9,5},{13... | collective-permute-start | bytes 737288 | tf_op jit(solution)/shard_map/ppermute | solution.py:12
  22.4 0.7 copy-start.8
  23.3 1.7 copy-start.7
  24.4 11.4 %collective-permute-start.2 = (f32[2,6,1,160,96]{4,3,2,1,0:T(8,128)}, f32[2,6,1,160,96]{4,3,2,1,0:T(8,128)}, u32[]{:S(2)}, u32[]{:S(2)}) collective-permute-start(f32[2,6,1,160,96]{4,3,2,1,0:T(8,128)} %slice_select_fusion), channel_id=1, source_target_pairs={{0,2},{2,0},{1,3},{3,1},{4,6},{6,4},{5,7},{7,5},{8,10},{10,8},{9,1... | collective-permute-start | bytes 2211848 | tf_op jit(solution)/shard_map/ppermute | solution.py:22
  35.8 1.5 copy-start.9
  42.5 7.1 %copy-start.5 = (f32[864,288,1,1]{0,1,2,3:T(8,128)S(1)}, f32[864,288,1,1]{0,1,2,3:T(8,128)}, u32[]{:S(2)}) copy-start(f32[864,288,1,1]{0,1,2,3:T(8,128)} %reshape.181) | copy-start | bytes 2985988
  49.5 6.2 %copy-start.12 = (f32[96]{0:T(128)S(1)}, f32[96]{0:T(128)}, u32[]{:S(2)}) copy-start(f32[96]{0:T(128)} %param.9) | copy-start | bytes 1156
  56.5 7.1 %copy-start.4 = (f32[864,288,1,1]{0,1,2,3:T(8,128)S(1)}, f32[864,288,1,1]{0,1,2,3:T(8,128)}, u32[]{:S(2)}) copy-start(f32[864,288,1,1]{0,1,2,3:T(8,128)} %reshape.180) | copy-start | bytes 2985988
  63.6 6.6 %copy-start.11 = (f32[96]{0:T(128)S(1)}, f32[96]{0:T(128)}, u32[]{:S(2)}) copy-start(f32[96]{0:T(128)} %param.12) | copy-start | bytes 1156
  63.6 11.7 %slice-start = ((s8[4816896]{0:T(1024)(128)(4,1)}), s8[4194304]{0:T(1024)(128)(4,1)S(1)}, s32[]{:S(2)}) async-start(s8[4816896]{0:T(1024)(128)(4,1)} %bitcast.118), calls=%async_computation | async-start | bytes 8388608
  70.2 5.1 %slice-start.1 = ((s8[4816896]{0:T(1024)(128)(4,1)}), s8[622592]{0:T(1024)(128)(4,1)S(1)}, s32[]{:S(2)}) async-start(s8[4816896]{0:T(1024)(128)(4,1)} %bitcast.118), calls=%async_computation.1 | async-start | bytes 1245184
  74.0 14.1 %collective-permute-start.3 = (f32[1,2,2,160,96]{4,3,2,1,0:T(8,128)}, f32[1,2,2,160,96]{4,3,2,1,0:T(8,128)}, u32[]{:S(2)}, u32[]{:S(2)}) collective-permute-start(f32[1,2,2,160,96]{4,3,2,1,0:T(8,128)} %slice.267), channel_id=1, source_target_pairs={{4,0},{8,4},{12,8},{16,12},{20,16},{24,20},{28,24},{5,1},{9,5},{13... | collective-permute-start | bytes 737288 | tf_op jit(solution)/shard_map/ppermute | solution.py:12
  84.4 3.0 %copy-start.6 = (f32[1,4,2,160,96]{4,3,2,1,0:T(8,128)S(1)}, f32[1,4,2,160,96]{4,3,2,1,0:T(8,128)}, u32[]{:S(2)}) copy-start(f32[1,4,2,160,96]{4,3,2,1,0:T(8,128)} %get-tuple-element.63) | copy-start | bytes 1474564
  90.0 13.1 %collective-permute-start.4 = (f32[1,6,1,160,96]{4,3,2,1,0:T(8,128)}, f32[1,6,1,160,96]{4,3,2,1,0:T(8,128)}, u32[]{:S(2)}, u32[]{:S(2)}) collective-permute-start(f32[1,6,1,160,96]{4,3,2,1,0:T(8,128)} %fusion.29), channel_id=1, source_target_pairs={{0,2},{2,0},{1,3},{3,1},{4,6},{6,4},{5,7},{7,5},{8,10},{10,8},{9,1... | collective-permute-start | bytes 1105928 | tf_op jit(solution)/shard_map/ppermute | solution.py:22
  107.9 7.0 %copy-start.3 = (f32[864,288,1,1]{0,1,2,3:T(8,128)S(1)}, f32[864,288,1,1]{0,1,2,3:T(8,128)}, u32[]{:S(2)}) copy-start(f32[864,288,1,1]{0,1,2,3:T(8,128)} %reshape.182) | copy-start | bytes 2985988
  114.9 6.3 %copy-start = (f32[1,4,2,160,96]{4,3,2,1,0:T(8,128)S(1)}, f32[1,4,2,160,96]{4,3,2,1,0:T(8,128)}, u32[]{:S(2)}) copy-start(f32[1,4,2,160,96]{4,3,2,1,0:T(8,128)} %param.7) | copy-start | bytes 1474564
  114.9 6.3 %copy-start.10 = (f32[96]{0:T(128)S(1)}, f32[96]{0:T(128)}, u32[]{:S(2)}) copy-start(f32[96]{0:T(128)} %param.10) | copy-start | bytes 1156
  122.3 1.4 copy-start.2
  132.7 3.0 %collective-permute-start.5 = (f32[8,1,326,96]{2,3,1,0:T(8,128)S(1)}, f32[8,1,326,96]{2,3,1,0:T(8,128)S(1)}, u32[]{:S(2)}, u32[]{:S(2)}) collective-permute-start(f32[8,1,326,96]{2,3,1,0:T(8,128)S(1)} %bitcast.130), channel_id=1, source_target_pairs={{0,2},{2,0},{1,3},{3,1},{4,6},{6,4},{5,7},{7,5},{8,10},{10,8},{9,1... | collective-permute-start | bytes 3004424 | tf_op jit(solution)/shard_map/ppermute | solution.py:90
  136.2 11.0 %collective-permute-start.6 = (f32[4,326,96]{1,2,0:T(8,128)S(1)}, f32[4,326,96]{1,2,0:T(8,128)S(1)}, u32[]{:S(2)}, u32[]{:S(2)}) collective-permute-start(f32[4,326,96]{1,2,0:T(8,128)S(1)} %dynamic-slice_bitcast_fusion), channel_id=1, source_target_pairs={{0,4},{2,10},{4,0},{6,14},{8,12},{10,2},{12,8},{14,6},{16,20},{18,... | collective-permute-start | bytes 1502216 | tf_op jit(solution)/shard_map/ppermute | solution.py:135
  147.3 8.2 %collective-permute-start.7 = (f32[2,326,96]{1,2,0:T(8,128)S(1)}, f32[2,326,96]{1,2,0:T(8,128)S(1)}, u32[]{:S(2)}, u32[]{:S(2)}) collective-permute-start(f32[2,326,96]{1,2,0:T(8,128)S(1)} %dynamic-slice_bitcast_fusion.1), channel_id=1, source_target_pairs={{0,8},{2,6},{4,12},{6,2},{8,0},{10,14},{12,4},{14,10},{16,24},{18,... | collective-permute-start | bytes 751112 | tf_op jit(solution)/shard_map/ppermute | solution.py:135
  155.6 9.3 %collective-permute-start.8 = (f32[1,326,96]{1,2,0:T(8,128)S(1)}, f32[1,326,96]{1,2,0:T(8,128)S(1)}, u32[]{:S(2)}, u32[]{:S(2)}) collective-permute-start(f32[1,326,96]{1,2,0:T(8,128)S(1)} %constant_dynamic-slice_fusion), channel_id=1, source_target_pairs={{0,16},{2,18},{4,20},{6,22},{8,24},{10,26},{12,28},{14,30},{16,0},... | collective-permute-start | bytes 375560 | tf_op jit(solution)/shard_map/ppermute | solution.py:135
  165.0 5.2 %collective-permute-start.9 = (f32[326,96]{0,1:T(8,128)S(1)}, f32[326,96]{0,1:T(8,128)S(1)}, u32[]{:S(2)}, u32[]{:S(2)}) collective-permute-start(f32[326,96]{0,1:T(8,128)S(1)} %add_bitcast_fusion), channel_id=1, source_target_pairs={{0,1},{1,0},{2,3},{3,2},{4,5},{5,4},{6,7},{7,6},{8,9},{9,8},{10,11... | collective-permute-start | bytes 375560 | tf_op jit(solution)/shard_map/ppermute | solution.py:90
  170.2 1.4 collective-permute-start.10
